TPU v7x, 512 devices: a whole 4x8x8 slice. The times are simulated.
512 devices in a mesh: dp: 2 (over core), section: 8 (over z), mem: 32 (over y, x).
Axes of the slice: x: 4, y: 8, z: 8, core: 2. Of those that a mesh axis runs over, the one named last changes fastest.
Arguments:
- qkv_rows: bfloat16 [8, 64, 128, 3072], P('section', ('dp', 'mem')), may hold values from -5 to 5
- grad_output: bfloat16 [8, 64, 128, 2048], P('section', ('dp', 'mem')), may hold values from -12 to 12
- memory_rows: bfloat16 [8, 256, 64, 1024], P('section', 'mem'), may hold values from -5 to 5
- shard_fill: int32 [8, 32], P('section', 'mem'), may hold values from 257 to 512, as said below
- block_ids: int32 [8, 64, 2, 8], P('section', ('dp', 'mem')), may hold values from 0 to 255, as said below
Outputs:
- upstream: bfloat16 [8, 64, 128, 3072], P('section', ('dp', 'mem'))
- memory_grad: bfloat16 [8, 256, 64, 1024], P('section', 'mem')
Inputs may be any that keep to these rules, and one draw needn't show every extreme that they name: `shard_fill`: memory tokens at or beyond a shard's fill are empty. In every section one shard is full and one holds 257 tokens. `block_ids`: each query block names 8 blocks of different shards; all query blocks of one sequence together name at most one distinct block of any one shard; every named block holds a live token.
All inputs are finite; a program needn't handle non-finite values.
Results may differ from a plain program's by a relative error of at most 0.011.
Values may be sent and summed in bfloat16 or wider, within the bound.
No kernel may reach another device: no remote copies, remote signals or barrier semaphores. Data moves between devices by JAX's collectives and lax.ppermute only.
A program may use at most 128 MiB of HBM per device.

v0:
```python
from functools import partial

import jax
import jax.numpy as jnp
from jax import lax
from jax.sharding import PartitionSpec as P

H = 16
KEY_VALUE_HEADS = 4
DH = 128
BLK = 64


NEG_FILL = -1e30


def passed_along(array, axis, by):
    devices = lax.axis_size(axis)
    pairs = [(i, i + by) for i in range(devices) if 0 <= i + by < devices]
    return lax.ppermute(array, axis, pairs)


def head_scores(key_mask, queries, key_rows):
    raw = jnp.einsum(
        "bighd,gbnd->bighn", queries, key_rows, preferred_element_type=jnp.float32
    ) * DH ** (-0.5)
    return jnp.where(key_mask[:, :, None, None, :], raw, NEG_FILL)


def head_forward(key_mask, pieces):
    queries, key_rows, value_rows = pieces
    scores = head_scores(key_mask, queries, key_rows)
    row_max = jnp.max(scores, axis=-1, keepdims=True)
    log_total = row_max + jnp.log(jnp.sum(jnp.exp(scores - row_max), axis=-1, keepdims=True))
    prob_bf = jnp.exp(scores - log_total).astype(jnp.bfloat16)
    attended = jnp.einsum(
        "bighn,gbnd->bighd", prob_bf, value_rows, preferred_element_type=jnp.float32
    ).astype(jnp.bfloat16)
    return (log_total, attended)


def head_backward(key_mask, pieces):
    queries, key_rows, value_rows, grad_rows, log_total, attended = pieces
    scores = head_scores(key_mask, queries, key_rows)
    weights = jnp.exp(scores - log_total)
    prob_bf = weights.astype(jnp.bfloat16)
    dprobs = jnp.einsum("bighd,gbnd->bighn", grad_rows, value_rows, preferred_element_type=jnp.float32)
    row_delta = jnp.sum(
        grad_rows.astype(jnp.float32) * attended.astype(jnp.float32), axis=-1, keepdims=True
    )
    dscores = (weights * (dprobs - row_delta)).astype(jnp.bfloat16)
    inv_root = DH ** (-0.5)
    grad_query = (
        jnp.einsum("bighn,gbnd->bighd", dscores, key_rows, preferred_element_type=jnp.float32)
        * inv_root
    )
    grad_key = (
        jnp.einsum("bighn,bighd->gbnd", dscores, queries, preferred_element_type=jnp.float32)
        * inv_root
    )
    grad_value = jnp.einsum(
        "bighn,bighd->gbnd", prob_bf, grad_rows, preferred_element_type=jnp.float32
    )
    return (grad_query, grad_key, grad_value)


def masks(slot_live, owner_shard, tokens):
    qblocks, topk = owner_shard.shape
    memory_len = topk * BLK
    live_len = jnp.take(slot_live, owner_shard.reshape(-1))
    live_mask = (jnp.arange(BLK)[None, :] < live_len[:, None]).reshape(qblocks, memory_len)
    row_pos = jnp.arange(qblocks)[:, None] * BLK + jnp.arange(BLK)[None, :]
    causal = jnp.arange(tokens)[None, None, :] <= row_pos[:, :, None]
    return jnp.concatenate(
        [jnp.broadcast_to(live_mask[:, None, :], (qblocks, BLK, memory_len)), causal], axis=-1
    )


def per_device(qkv_rows, grad_output, memory_rows, shard_fill, block_ids):
    shards = lax.axis_size("mem")
    groups = H // KEY_VALUE_HEADS
    rows_here = qkv_rows[0, 0]
    tokens = rows_here.shape[0]
    ids_here = block_ids[0, 0]
    qblocks, topk = ids_here.shape
    memory_len = topk * BLK
    held_blocks = memory_rows.shape[1]
    queries = rows_here[:, : H * DH].reshape(qblocks, BLK, KEY_VALUE_HEADS, groups, DH)
    keys_local = rows_here[:, H * DH : (H + KEY_VALUE_HEADS) * DH].reshape(
        tokens, KEY_VALUE_HEADS, DH
    )
    values_local = rows_here[:, (H + KEY_VALUE_HEADS) * DH :].reshape(tokens, KEY_VALUE_HEADS, DH)
    grad_rows = grad_output[0, 0].reshape(qblocks, BLK, KEY_VALUE_HEADS, groups, DH)
    owner_shard = ids_here // held_blocks
    slot_index = ids_here % held_blocks
    shard_ids = jnp.arange(shards, dtype=jnp.int32)
    hits = owner_shard[:, :, None] == shard_ids[None, None, :]
    request = jnp.max(jnp.where(hits, slot_index[:, :, None], -1), axis=(0, 1))
    asks = jnp.stack([request, jnp.broadcast_to(shard_fill[0, 0], (shards,))], axis=1)
    answers = lax.all_to_all(asks, "mem", split_axis=0, concat_axis=0, tiled=True)
    wanted = answers[:, 0]
    fills = answers[:, 1]
    slot_live = jnp.where(request >= 0, jnp.clip(fills - request * BLK, 0, BLK), 0)
    key_mask = masks(slot_live, owner_shard, tokens)
    memory_here = memory_rows[0]
    width = KEY_VALUE_HEADS * DH
    wanted_hot = (wanted[:, None] == jnp.arange(held_blocks, dtype=jnp.int32)[None, :]).astype(
        jnp.bfloat16
    )
    entry_hot = (owner_shard.reshape(-1)[:, None] == shard_ids[None, :]).astype(jnp.bfloat16)
    per_chunk = 2
    chunks = KEY_VALUE_HEADS // per_chunk
    span = per_chunk * DH
    query_parts, key_parts, value_parts, owned_parts, sent_grads = [], [], [], [], []
    for chunk in range(chunks):
        first = chunk * per_chunk
        lo = first * DH
        memory_chunk = jnp.concatenate(
            [memory_here[:, :, lo : lo + span], memory_here[:, :, width + lo : width + lo + span]],
            axis=-1,
        )
        payload = memory_chunk.at[jnp.maximum(wanted, 0)].get(mode="promise_in_bounds")
        if chunk >= 2:
            payload, sent_grads[chunk - 2] = lax.optimization_barrier(
                (payload, sent_grads[chunk - 2])
            )
        slots = lax.all_to_all(payload, "mem", split_axis=0, concat_axis=0, tiled=True)
        chosen = jnp.einsum(
            "es,stx->etx", entry_hot, slots, preferred_element_type=jnp.bfloat16
        ).reshape(qblocks, memory_len, 2, per_chunk, DH)
        mem_keys = jnp.transpose(chosen[:, :, 0], (2, 0, 1, 3))
        mem_values = jnp.transpose(chosen[:, :, 1], (2, 0, 1, 3))
        local_keys = jnp.transpose(keys_local[:, first : first + per_chunk], (1, 0, 2))
        local_values = jnp.transpose(values_local[:, first : first + per_chunk], (1, 0, 2))
        key_rows = jnp.concatenate(
            [mem_keys, jnp.broadcast_to(local_keys[:, None], (per_chunk, qblocks, tokens, DH))],
            axis=2,
        )
        value_rows = jnp.concatenate(
            [mem_values, jnp.broadcast_to(local_values[:, None], (per_chunk, qblocks, tokens, DH))],
            axis=2,
        )
        queries_chunk = queries[:, :, first : first + per_chunk]
        grads_chunk = grad_rows[:, :, first : first + per_chunk]
        log_total, attended = head_forward(key_mask, (queries_chunk, key_rows, value_rows))
        grad_query, grad_key, grad_value = head_backward(
            key_mask,
            (queries_chunk, key_rows, value_rows, grads_chunk, log_total, attended),
        )
        query_parts.append(grad_query.reshape(tokens, per_chunk * groups * DH))
        key_parts.append(
            jnp.transpose(jnp.sum(grad_key[:, :, memory_len:], axis=1), (1, 0, 2)).reshape(
                tokens, span
            )
        )
        value_parts.append(
            jnp.transpose(jnp.sum(grad_value[:, :, memory_len:], axis=1), (1, 0, 2)).reshape(
                tokens, span
            )
        )
        entry_grads = jnp.stack(
            [grad_key[:, :, :memory_len], grad_value[:, :, :memory_len]], axis=0
        )
        entry_grads = jnp.transpose(
            entry_grads.reshape(2, per_chunk, qblocks * topk, BLK, DH), (2, 3, 0, 1, 4)
        ).reshape(qblocks * topk, BLK, 2 * span)
        slot_grads = jnp.einsum(
            "es,etx->stx",
            entry_hot.astype(jnp.float32),
            entry_grads,
            precision=lax.Precision.HIGHEST,
            preferred_element_type=jnp.float32,
        ).astype(jnp.bfloat16)
        sent_grads.append(slot_grads)
    for chunk in range(chunks):
        received = lax.all_to_all(
            sent_grads[chunk], "mem", split_axis=0, concat_axis=0, tiled=True
        )
        owned = jnp.einsum(
            "rj,rtx->jtx", wanted_hot, received, preferred_element_type=jnp.float32
        )
        partner = lax.ppermute(owned, "dp", [(0, 1), (1, 0)])
        owned_parts.append(owned + partner)
    section_grads = jnp.concatenate(query_parts + key_parts + value_parts, axis=-1).astype(
        jnp.bfloat16
    )
    upstream = passed_along(section_grads[None, None], "section", -1)
    summed = jnp.concatenate(
        [part[:, :, :span] for part in owned_parts] + [part[:, :, span:] for part in owned_parts],
        axis=-1,
    )
    memory_grad = summed.astype(jnp.bfloat16)[None]
    return (upstream, memory_grad)


def solution(mesh):
    placed = (
        P("section", ("dp", "mem"), None, None),
        P("section", ("dp", "mem"), None, None),
        P("section", "mem", None, None),
        P("section", "mem"),
        P("section", ("dp", "mem"), None, None),
    )
    return jax.shard_map(
        per_device,
        mesh=mesh,
        in_specs=placed,
        out_specs=(P("section", ("dp", "mem"), None, None), P("section", "mem", None, None)),
        check_vma=False,
    )
```

profile of v0, /device:TPU:1, one launch (start us, length us, event | category | flops | bytes accessed | tf_op | source)
XLA Modules:
  0.0 255.9 jit_solution(12357632226809152883)
XLA Ops:
  2.8 10.5 %all-to-all-start = ((s32[32,1,2]{2,1,0:T(1,128)}), s32[32,1,2]{2,1,0:T(1,128)S(1)}, u32[]{:S(2)}, u32[]{:S(2)}) async-start(s32[32,1,2]{2,1,0:T(1,128)} %copy.137), calls=%async_computation | async-start | bytes 32768 | tf_op jit(solution)/shard_map/all_to_all | solution.py:100
  16.1 5.7 %all-to-all-done = s32[32,1,2]{2,1,0:T(1,128)S(1)} async-done(((s32[32,1,2]{2,1,0:T(1,128)}), s32[32,1,2]{2,1,0:T(1,128)S(1)}, u32[]{:S(2)}, u32[]{:S(2)}) %all-to-all-start) | async-done | bytes 288 | tf_op jit(solution)/shard_map/all_to_all | solution.py:100
  25.0 4.1 %all-to-all-start.2 = ((bf16[32,64,512]{2,1,0:T(8,128)(2,1)}), bf16[32,64,512]{2,1,0:T(8,128)(2,1)S(1)}, u32[]{:S(2)}, u32[]{:S(2)}) async-start(bf16[32,64,512]{2,1,0:T(8,128)(2,1)} %gather_fusion.2), calls=%async_computation.2 | async-start | bytes 4194304 | tf_op jit(solution)/shard_map/all_to_all | solution.py:127
  40.2 35.9 %all-to-all-done.2 = bf16[32,64,512]{2,1,0:T(8,128)(2,1)S(1)} async-done(((bf16[32,64,512]{2,1,0:T(8,128)(2,1)}), bf16[32,64,512]{2,1,0:T(8,128)(2,1)S(1)}, u32[]{:S(2)}, u32[]{:S(2)}) %all-to-all-start.2) | async-done | bytes 2097184 | tf_op jit(solution)/shard_map/all_to_all | solution.py:127
  77.5 7.6 %all-to-all-start.1 = ((bf16[32,64,512]{2,1,0:T(8,128)(2,1)}), bf16[32,64,512]{2,1,0:T(8,128)(2,1)S(1)}, u32[]{:S(2)}, u32[]{:S(2)}) async-start(bf16[32,64,512]{2,1,0:T(8,128)(2,1)} %gather_fusion), calls=%async_computation.1 | async-start | bytes 4194304 | tf_op jit(solution)/shard_map/all_to_all | solution.py:127
  89.6 3.1 %fusion.14 = bf16[16,64,512]{2,0,1:T(8,128)(2,1)S(1)} fusion(bf16[32,64,512]{2,1,0:T(8,128)(2,1)} %copy-done.1, s32[16]{0:T(128)S(1)} %and_select_fusion.4), kind=kOutput, calls=%fused_computation.27 | convolution fusion | flops 33554944 | bytes 3145792 | tf_op jit(solution)/shard_map/es,stx->etx/dot_general | solution.py:128
  104.8 2.4 maximum_bitcast_fusion.1
  107.1 14.7 %reshape.429 = f32[16,64,512]{2,1,0:T(8,128)} reshape(f32[16,64,2,2,128]{4,3,2,1,0:T(2,128)} %maximum_bitcast_fusion.1) | data formatting | bytes 4194304 | tf_op jit(solution)/shard_map/reshape | solution.py:166
  121.8 4.5 %fusion.21 = bf16[32,64,512]{2,0,1:T(8,128)(2,1)S(1)} fusion(f32[16,64,512]{2,1,0:T(8,128)} %reshape.429, s32[16]{0:T(128)S(1)} %and_select_fusion.4), kind=kOutput, calls=%fused_computation.32 | convolution fusion | flops 202375680 | bytes 4194368 | tf_op jit(solution)/shard_map/es,etx->stx/dot_general | solution.py:167
  126.3 2.5 copy.181
  128.8 2.4 all-to-all-done.1
  132.4 7.5 %all-to-all-start.4 = ((bf16[32,64,512]{2,1,0:T(8,128)(2,1)}), bf16[32,64,512]{2,1,0:T(8,128)(2,1)S(1)}, u32[]{:S(2)}, u32[]{:S(2)}) async-start(bf16[32,64,512]{2,1,0:T(8,128)(2,1)} %copy.181), calls=%async_computation.4 | async-start | bytes 4194304 | tf_op jit(solution)/shard_map/all_to_all | solution.py:176
  139.9 3.1 %fusion.16 = bf16[16,64,512]{2,0,1:T(8,128)(2,1)S(1)} fusion(bf16[32,64,512]{2,1,0:T(8,128)(2,1)} %copy-done, s32[16]{0:T(128)S(1)} %and_select_fusion.4), kind=kOutput, calls=%fused_computation.29 | convolution fusion | flops 33554944 | bytes 3145792 | tf_op jit(solution)/shard_map/es,stx->etx/dot_general | solution.py:128
  144.5 2.2 reshape.423
  157.5 2.4 maximum_bitcast_fusion
  159.9 3.9 %reshape.428 = f32[16,64,512]{2,1,0:T(8,128)} reshape(f32[16,64,2,2,128]{4,3,2,1,0:T(2,128)} %maximum_bitcast_fusion) | data formatting | bytes 4194304 | tf_op jit(solution)/shard_map/reshape | solution.py:166
  163.8 4.4 %fusion.18 = bf16[32,64,512]{2,0,1:T(8,128)(2,1)S(1)} fusion(f32[16,64,512]{2,1,0:T(8,128)} %reshape.428, s32[16]{0:T(128)S(1)} %and_select_fusion.4), kind=kOutput, calls=%fused_computation.31 | convolution fusion | flops 202375680 | bytes 4194368 | tf_op jit(solution)/shard_map/es,etx->stx/dot_general | solution.py:167
  168.3 2.5 copy.176
  170.8 15.5 %all-to-all-done.4 = bf16[32,64,512]{2,1,0:T(8,128)(2,1)S(1)} async-done(((bf16[32,64,512]{2,1,0:T(8,128)(2,1)}), bf16[32,64,512]{2,1,0:T(8,128)(2,1)S(1)}, u32[]{:S(2)}, u32[]{:S(2)}) %all-to-all-start.4) | async-done | bytes 2097184 | tf_op jit(solution)/shard_map/all_to_all | solution.py:176
  186.2 7.3 %all-to-all-start.3 = ((bf16[32,64,512]{2,1,0:T(8,128)(2,1)}), bf16[32,64,512]{2,1,0:T(8,128)(2,1)}, u32[]{:S(2)}, u32[]{:S(2)}) async-start(bf16[32,64,512]{2,1,0:T(8,128)(2,1)} %copy.176), calls=%async_computation.3 | async-start | bytes 4194304 | tf_op jit(solution)/shard_map/all_to_all | solution.py:176
  212.5 5.5 %collective-permute-start.2 = (f32[8,64,512]{2,0,1:T(8,128)S(1)}, f32[8,64,512]{2,0,1:T(8,128)S(1)}, u32[]{:S(2)}, u32[]{:S(2)}) collective-permute-start(f32[8,64,512]{2,0,1:T(8,128)S(1)} %fusion.6), channel_id=1, source_target_pairs={{0,256},{256,0},{1,257},{257,1},{2,258},{258,2},{3,259},{259,3},{4... | collective-permute-start | bytes 3145736 | tf_op jit(solution)/shard_map/ppermute | solution.py:182
  222.0 17.4 %all-to-all-done.3 = bf16[32,64,512]{2,1,0:T(8,128)(2,1)} async-done(((bf16[32,64,512]{2,1,0:T(8,128)(2,1)}), bf16[32,64,512]{2,1,0:T(8,128)(2,1)}, u32[]{:S(2)}, u32[]{:S(2)}) %all-to-all-start.3) | async-done | bytes 2097184 | tf_op jit(solution)/shard_map/all_to_all | solution.py:176
  239.4 2.8 %fusion.10 = f32[8,64,512]{2,0,1:T(8,128)S(1)} fusion(bf16[32,64,512]{2,1,0:T(8,128)(2,1)} %all-to-all-done.3, s32[32]{0:T(128)S(1)} %copy-done.24), kind=kOutput, calls=%fused_computation.23 | convolution fusion | flops 16777472 | bytes 3145856 | tf_op jit(solution)/shard_map/rj,rtx->jtx/dot_general | solution.py:179
  242.2 7.1 %collective-permute-start.1 = (f32[8,64,512]{2,0,1:T(8,128)S(1)}, f32[8,64,512]{2,0,1:T(8,128)S(1)}, u32[]{:S(2)}, u32[]{:S(2)}) collective-permute-start(f32[8,64,512]{2,0,1:T(8,128)S(1)} %fusion.10), channel_id=1, source_target_pairs={{0,256},{256,0},{1,257},{257,1},{2,258},{258,2},{3,259},{259,3},{4... | collective-permute-start | bytes 3145736 | tf_op jit(solution)/shard_map/ppermute | solution.py:182
  (169 shorter events, 78.7 us)
Async XLA Ops:
  2.1 14.0 %copy-start.23 = (s32[32]{0:T(128)}, s32[32]{0:T(128)S(1)}, u32[]{:S(2)}) copy-start(s32[32]{0:T(128)S(1)} %select_reduce_fusion) | copy-start | bytes 388
  2.8 19.0 %all-to-all-start = ((s32[32,1,2]{2,1,0:T(1,128)}), s32[32,1,2]{2,1,0:T(1,128)S(1)}, u32[]{:S(2)}, u32[]{:S(2)}) async-start(s32[32,1,2]{2,1,0:T(1,128)} %copy.137), calls=%async_computation | async-start | bytes 32768 | tf_op jit(solution)/shard_map/all_to_all | solution.py:100
  25.0 4.2 %copy-start.25 = (s32[1,1,2,8]{3,2,1,0:T(2,128)S(1)}, s32[1,1,2,8]{3,2,1,0:T(2,128)}, u32[]{:S(2)}) copy-start(s32[1,1,2,8]{3,2,1,0:T(2,128)} %param.9) | copy-start | bytes 196
  25.0 51.2 %all-to-all-start.2 = ((bf16[32,64,512]{2,1,0:T(8,128)(2,1)}), bf16[32,64,512]{2,1,0:T(8,128)(2,1)S(1)}, u32[]{:S(2)}, u32[]{:S(2)}) async-start(bf16[32,64,512]{2,1,0:T(8,128)(2,1)} %gather_fusion.2), calls=%async_computation.2 | async-start | bytes 4194304 | tf_op jit(solution)/shard_map/all_to_all | solution.py:127
  40.2 44.9 %copy-start.27 = (s32[16]{0:T(128)S(1)}, s32[16]{0:T(128)}, u32[]{:S(2)}) copy-start(s32[16]{0:T(128)} %squeeze.32) | copy-start | bytes 196
  40.2 45.0 %copy-start.10 = (bf16[1,1,128,2048]{3,2,1,0:T(8,128)(2,1)S(1)}, bf16[1,1,128,2048]{3,2,1,0:T(8,128)(2,1)}, u32[]{:S(2)}) copy-start(bf16[1,1,128,2048]{3,2,1,0:T(8,128)(2,1)} %param.6) | copy-start | bytes 1572868
  76.1 1.3 copy-start.1
  77.5 53.7 %all-to-all-start.1 = ((bf16[32,64,512]{2,1,0:T(8,128)(2,1)}), bf16[32,64,512]{2,1,0:T(8,128)(2,1)S(1)}, u32[]{:S(2)}, u32[]{:S(2)}) async-start(bf16[32,64,512]{2,1,0:T(8,128)(2,1)} %gather_fusion), calls=%async_computation.1 | async-start | bytes 4194304 | tf_op jit(solution)/shard_map/all_to_all | solution.py:127
  86.5 13.2 %copy-start.4 = (bf16[2,64,2,4,128]{4,3,2,1,0:T(4,128)(2,1)}, bf16[2,64,2,4,128]{4,3,2,1,0:T(4,128)(2,1)S(1)}, u32[]{:S(2)}) copy-start(bf16[2,64,2,4,128]{4,3,2,1,0:T(4,128)(2,1)S(1)} %get-tuple-element.26) | copy-start | bytes 786436
  95.6 1.7 copy-start.16
  95.6 1.7 copy-start.21
  96.5 1.5 copy-start.11
  101.1 1.9 copy-start.5
  131.1 1.3 copy-start
  132.4 53.8 %all-to-all-start.4 = ((bf16[32,64,512]{2,1,0:T(8,128)(2,1)}), bf16[32,64,512]{2,1,0:T(8,128)(2,1)S(1)}, u32[]{:S(2)}, u32[]{:S(2)}) async-start(bf16[32,64,512]{2,1,0:T(8,128)(2,1)} %copy.181), calls=%async_computation.4 | async-start | bytes 4194304 | tf_op jit(solution)/shard_map/all_to_all | solution.py:176
  146.7 2.2 copy-start.15
  146.7 2.2 copy-start.22
  148.9 1.7 copy-start.19
  170.8 22.7 %copy-start.18 = (bf16[2,2,128,128]{3,2,0,1:T(8,128)(2,1)S(1)}, bf16[2,2,128,128]{3,2,0,1:T(8,128)(2,1)}, u32[]{:S(2)}) copy-start(bf16[2,2,128,128]{3,2,0,1:T(8,128)(2,1)} %copy-done.17) | copy-start | bytes 393220
  186.2 53.2 %all-to-all-start.3 = ((bf16[32,64,512]{2,1,0:T(8,128)(2,1)}), bf16[32,64,512]{2,1,0:T(8,128)(2,1)}, u32[]{:S(2)}, u32[]{:S(2)}) async-start(bf16[32,64,512]{2,1,0:T(8,128)(2,1)} %copy.176), calls=%async_computation.3 | async-start | bytes 4194304 | tf_op jit(solution)/shard_map/all_to_all | solution.py:176
  202.9 8.4 %copy-start.24 = (s32[32]{0:T(128)S(1)}, s32[32]{0:T(128)}, u32[]{:S(2)}) copy-start(s32[32]{0:T(128)} %get-tuple-element.34) | copy-start | bytes 388
  212.5 36.8 %collective-permute-start.2 = (f32[8,64,512]{2,0,1:T(8,128)S(1)}, f32[8,64,512]{2,0,1:T(8,128)S(1)}, u32[]{:S(2)}, u32[]{:S(2)}) collective-permute-start(f32[8,64,512]{2,0,1:T(8,128)S(1)} %fusion.6), channel_id=1, source_target_pairs={{0,256},{256,0},{1,257},{257,1},{2,258},{258,2},{3,259},{259,3},{4... | collective-permute-start | bytes 3145736 | tf_op jit(solution)/shard_map/ppermute | solution.py:182
  220.7 28.6 %collective-permute-start = (bf16[1,1,128,3072]{3,2,1,0:T(8,128)(2,1)}, bf16[1,1,128,3072]{3,2,1,0:T(8,128)(2,1)}, u32[]{:S(2)}, u32[]{:S(2)}) collective-permute-start(bf16[1,1,128,3072]{3,2,1,0:T(8,128)(2,1)} %constant_dynamic-update-slice_fusion), channel_id=1, source_target_pairs={{32,0},{64,32},{96,64},{128,96},{160,128},{192,160},{224,192},{33,... | collective-permute-start | bytes 2359304 | tf_op jit(solution)/shard_map/ppermute | solution.py:20
  242.2 9.4 %collective-permute-start.1 = (f32[8,64,512]{2,0,1:T(8,128)S(1)}, f32[8,64,512]{2,0,1:T(8,128)S(1)}, u32[]{:S(2)}, u32[]{:S(2)}) collective-permute-start(f32[8,64,512]{2,0,1:T(8,128)S(1)} %fusion.10), channel_id=1, source_target_pairs={{0,256},{256,0},{1,257},{257,1},{2,258},{258,2},{3,259},{259,3},{4... | collective-permute-start | bytes 3145736 | tf_op jit(solution)/shard_map/ppermute | solution.py:182
  (12 other events, 11.8 us)
where the time goes:
time: 260 us; the launch traced here: 256 us
  waiting for transfers between devices  78.8 us (30%)
  local copies, waits for them, and re-layouts  77.5 us (30%)
  starting transfers between devices  50.9 us (20%)
  matrix products  30.5 us (12%)
  other arithmetic  15.9 us (6%)
    all_to_all x2, waiting for transfers between devices, per_device(): lax.all_to_all(payload, 'mem', split_axis=0, concat_axis=0, tiled=True)  38.3 us
    all_to_all x2, waiting for transfers between devices, per_device(): lax.all_to_all(sent_grads[chunk], 'mem', split_axis=0, concat_axis=0, til...  32.9 us
    reshape x2, local copies, waits for them, and re-layouts, per_device(): entry_grads = jnp.transpose(entry_grads.reshape(2, per_chunk, qblocks * t...  18.6 us
    all_to_all x2, starting transfers between devices, per_device(): lax.all_to_all(sent_grads[chunk], 'mem', split_axis=0, concat_axis=0, til...  14.7 us
    unnamed x67, local copies, waits for them, and re-layouts  13.9 us
    ppermute x2, starting transfers between devices, per_device(): partner = lax.ppermute(owned, 'dp', [(0, 1), (1, 0)])  12.6 us
    all_to_all x2, starting transfers between devices, per_device(): lax.all_to_all(payload, 'mem', split_axis=0, concat_axis=0, tiled=True)  11.8 us
    all_to_all x1, starting transfers between devices, per_device(): lax.all_to_all(asks, 'mem', split_axis=0, concat_axis=0, tiled=True)  10.5 us
  transfers between devices with their start and end apart: 8, of which 6 were waited for; matrix products, arithmetic and copies ran while one was open for 42% of the time, Pallas kernels for 0%

commit v1 on v0

--- a/solution.py
+++ b/solution.py
@@ -107,7 +107,9 @@
     wanted_hot = (wanted[:, None] == jnp.arange(held_blocks, dtype=jnp.int32)[None, :]).astype(
         jnp.bfloat16
     )
-    entry_hot = (owner_shard.reshape(-1)[:, None] == shard_ids[None, :]).astype(jnp.bfloat16)
+    owner_flat = owner_shard.reshape(-1)
+    key_slot = jnp.sum(jnp.where(hits, jnp.arange(topk, dtype=jnp.int32)[None, :, None], 0), axis=1)
+    present = jnp.any(hits, axis=1)
     per_chunk = 2
     chunks = KEY_VALUE_HEADS // per_chunk
     span = per_chunk * DH
@@ -125,9 +127,13 @@
                 (payload, sent_grads[chunk - 2])
             )
         slots = lax.all_to_all(payload, "mem", split_axis=0, concat_axis=0, tiled=True)
-        chosen = jnp.einsum(
-            "es,stx->etx", entry_hot, slots, preferred_element_type=jnp.bfloat16
-        ).reshape(qblocks, memory_len, 2, per_chunk, DH)
+        if chunk >= 1:
+            slots, sent_grads[chunk - 1] = lax.optimization_barrier(
+                (slots, sent_grads[chunk - 1])
+            )
+        chosen = slots.at[owner_flat].get(mode="promise_in_bounds").reshape(
+            qblocks, memory_len, 2, per_chunk, DH
+        )
         mem_keys = jnp.transpose(chosen[:, :, 0], (2, 0, 1, 3))
         mem_values = jnp.transpose(chosen[:, :, 1], (2, 0, 1, 3))
         local_keys = jnp.transpose(keys_local[:, first : first + per_chunk], (1, 0, 2))
@@ -164,12 +170,14 @@
         entry_grads = jnp.transpose(
             entry_grads.reshape(2, per_chunk, qblocks * topk, BLK, DH), (2, 3, 0, 1, 4)
         ).reshape(qblocks * topk, BLK, 2 * span)
-        slot_grads = jnp.einsum(
-            "es,etx->stx",
-            entry_hot.astype(jnp.float32),
-            entry_grads,
-            precision=lax.Precision.HIGHEST,
-            preferred_element_type=jnp.float32,
+        by_block = entry_grads.reshape(qblocks, topk, BLK, 2 * span)
+        slot_grads = sum(
+            jnp.where(
+                present[block][:, None, None],
+                by_block[block].at[key_slot[block]].get(mode="promise_in_bounds"),
+                jnp.float32(0.0),
+            )
+            for block in range(qblocks)
         ).astype(jnp.bfloat16)
         sent_grads.append(slot_grads)
     for chunk in range(chunks):

time: 260 us -> 256 us (0.985)
  other arithmetic: 15.9 us -> 34.9 us
  matrix products: 30.5 us -> 15.5 us
  local copies, waits for them, and re-layouts: 77.5 us -> 72.5 us
  waiting for transfers between devices: 78.8 us -> 74.9 us
    convert_element_type x0 -> x2, other arithmetic: none -> 21.8 us  [per_device(): slot_grads = sum((jnp.where(present[block][:, None, None], by_block[block...]
    reshape x4 -> x2, local copies, waits for them, and re-layouts: 22.1 us -> 2 us  [per_device(): slots.at[owner_flat].get(mode='promise_in_bounds')]
    gather x0 -> x6, local copies, waits for them, and re-layouts: none -> 15.9 us  [the longest x4 11.8 us: per_device(): by_block[block].at[key_slot[block]].get(mode='promise_in_bounds')]
    dot_general x4 -> x0, matrix products: 15 us -> none  [the longest x2 8.9 us: per_device(): jnp.einsum('es,etx->stx', entry_hot.astype(jnp.float32), entry_grads, pre...]
    squeeze x0 -> x4, local copies, waits for them, and re-layouts: none -> 5.81 us  [per_device(): by_block[block].at[key_slot[block]].get(mode='promise_in_bounds')]
    convert_element_type x2 -> x0, local copies, waits for them, and re-layouts: 4.97 us -> none  [per_device(): slot_grads = jnp.einsum('es,etx->stx', entry_hot.astype(jnp.float32), ent...]
    slice x0 -> x2, local copies, waits for them, and re-layouts: none -> 3.61 us  [per_device(): by_block[block].at[key_slot[block]].get(mode='promise_in_bounds')]
    unnamed x67 -> x77, local copies, waits for them, and re-layouts: 13.9 us -> 10.4 us
  transfers between devices with their start and end apart: 8 -> 8, of which waited for: 6 -> 6; matrix products, arithmetic and copies ran while one was open for 42% -> 44% of each run, Pallas kernels for 0% -> 0%
where the time goes in v1:
time: 256 us; the launch traced here: 251 us
  waiting for transfers between devices  74.9 us (29%)
  local copies, waits for them, and re-layouts  72.5 us (28%)
  starting transfers between devices  50.6 us (20%)
  other arithmetic  34.9 us (14%)
  matrix products  15.5 us (6%)
    all_to_all x2, waiting for transfers between devices, per_device(): lax.all_to_all(payload, 'mem', split_axis=0, concat_axis=0, tiled=True)  36.2 us
    all_to_all x2, waiting for transfers between devices, per_device(): lax.all_to_all(sent_grads[chunk], 'mem', split_axis=0, concat_axis=0, til...  31.4 us
    convert_element_type x2, other arithmetic, per_device(): slot_grads = sum((jnp.where(present[block][:, None, None], by_block[block...  21.8 us
    all_to_all x2, starting transfers between devices, per_device(): lax.all_to_all(sent_grads[chunk], 'mem', split_axis=0, concat_axis=0, til...  14.7 us
    ppermute x2, starting transfers between devices, per_device(): partner = lax.ppermute(owned, 'dp', [(0, 1), (1, 0)])  12.6 us
    gather x4, local copies, waits for them, and re-layouts, per_device(): by_block[block].at[key_slot[block]].get(mode='promise_in_bounds')  11.8 us
    all_to_all x2, starting transfers between devices, per_device(): lax.all_to_all(payload, 'mem', split_axis=0, concat_axis=0, tiled=True)  11.5 us
    all_to_all x1, starting transfers between devices, per_device(): lax.all_to_all(asks, 'mem', split_axis=0, concat_axis=0, tiled=True)  10.5 us
  transfers between devices with their start and end apart: 8, of which 6 were waited for; matrix products, arithmetic and copies ran while one was open for 44% of the time, Pallas kernels for 0%

profile of v1, /device:TPU:1, one launch (start us, length us, event | category | flops | bytes accessed | tf_op | source)
XLA Modules:
  0.0 250.8 jit_solution(17331312027608068078)
XLA Ops:
  2.8 10.5 %all-to-all-start = ((s32[32,1,2]{2,1,0:T(1,128)}), s32[32,1,2]{2,1,0:T(1,128)S(1)}, u32[]{:S(2)}, u32[]{:S(2)}) async-start(s32[32,1,2]{2,1,0:T(1,128)} %copy.121), calls=%async_computation | async-start | bytes 32768 | tf_op jit(solution)/shard_map/all_to_all | solution.py:100
  15.3 6.5 %all-to-all-done = s32[32,1,2]{2,1,0:T(1,128)S(1)} async-done(((s32[32,1,2]{2,1,0:T(1,128)}), s32[32,1,2]{2,1,0:T(1,128)S(1)}, u32[]{:S(2)}, u32[]{:S(2)}) %all-to-all-start) | async-done | bytes 288 | tf_op jit(solution)/shard_map/all_to_all | solution.py:100
  24.4 4.2 %all-to-all-start.1 = ((bf16[32,64,512]{2,1,0:T(8,128)(2,1)}), bf16[32,64,512]{2,1,0:T(8,128)(2,1)S(1)}, u32[]{:S(2)}, u32[]{:S(2)}) async-start(bf16[32,64,512]{2,1,0:T(8,128)(2,1)} %gather_fusion), calls=%async_computation.1 | async-start | bytes 4194304 | tf_op jit(solution)/shard_map/all_to_all | solution.py:129
  42.2 2.2 gather_fusion.3
  44.4 31.3 %all-to-all-done.1 = bf16[32,64,512]{2,1,0:T(8,128)(2,1)S(1)} async-done(((bf16[32,64,512]{2,1,0:T(8,128)(2,1)}), bf16[32,64,512]{2,1,0:T(8,128)(2,1)S(1)}, u32[]{:S(2)}, u32[]{:S(2)}) %all-to-all-start.1) | async-done | bytes 2097184 | tf_op jit(solution)/shard_map/all_to_all | solution.py:129
  75.6 7.4 %all-to-all-start.2 = ((bf16[32,64,512]{2,1,0:T(8,128)(2,1)}), bf16[32,64,512]{2,1,0:T(8,128)(2,1)}, u32[]{:S(2)}, u32[]{:S(2)}) async-start(bf16[32,64,512]{2,1,0:T(8,128)(2,1)} %gather_fusion.3), calls=%async_computation.2 | async-start | bytes 4194304 | tf_op jit(solution)/shard_map/all_to_all | solution.py:129
  100.4 2.1 squeeze.60
  102.5 2.9 %gather_fusion.5 = f32[32,64,512]{2,1,0:T(8,128)} fusion(f32[8,64,512]{2,1,0:T(8,128)S(1)} %squeeze.60, s32[1024]{0:T(1024)} %get-tuple-element.58), kind=kCustom, calls=%fused_computation.5 | custom fusion | bytes 8388736 | tf_op jit(solution)/shard_map/gather | solution.py:177
  105.4 3.1 %gather_fusion.4 = f32[32,64,512]{2,1,0:T(8,128)} fusion(f32[8,64,512]{2,1,0:T(8,128)S(1)} %squeeze.58, s32[1024]{0:T(1024)} %get-tuple-element.59), kind=kCustom, calls=%fused_computation.4 | custom fusion | bytes 8388736 | tf_op jit(solution)/shard_map/gather | solution.py:177
  108.5 15.6 %add_convert_fusion.1 = bf16[32,64,512]{2,1,0:T(8,128)(2,1)} fusion(f32[32,64,512]{2,1,0:T(8,128)} %gather_fusion.5, f32[32,64,512]{2,1,0:T(8,128)} %gather_fusion.4, pred[32]{0:T(512)(128)(4,1)S(1)} %copy-done.27, pred[32]{0:T(512)(128)(4,1)S(1)} %copy-done.26), kind=kLoop, calls=%fused_computation.10 | loop fusion | flops 4194304 | bytes 10485824 | tf_op jit(solution)/shard_map/convert_element_type | solution.py:181
  124.1 4.9 %all-to-all-done.2 = bf16[32,64,512]{2,1,0:T(8,128)(2,1)} async-done(((bf16[32,64,512]{2,1,0:T(8,128)(2,1)}), bf16[32,64,512]{2,1,0:T(8,128)(2,1)}, u32[]{:S(2)}, u32[]{:S(2)}) %all-to-all-start.2) | async-done | bytes 2097184 | tf_op jit(solution)/shard_map/all_to_all | solution.py:129
  129.0 7.6 %all-to-all-start.3 = ((bf16[32,64,512]{2,1,0:T(8,128)(2,1)}), bf16[32,64,512]{2,1,0:T(8,128)(2,1)}, u32[]{:S(2)}, u32[]{:S(2)}) async-start(bf16[32,64,512]{2,1,0:T(8,128)(2,1)} %add_convert_fusion.1), calls=%async_computation.3 | async-start | bytes 4194304 | tf_op jit(solution)/shard_map/all_to_all | solution.py:184
  136.6 2.3 gather_fusion.6
  152.5 2.1 squeeze.65
  154.5 2.9 %gather_fusion.8 = f32[32,64,512]{2,1,0:T(8,128)} fusion(f32[8,64,512]{2,1,0:T(8,128)S(1)} %squeeze.65, s32[1024]{0:T(1024)} %get-tuple-element.58), kind=kCustom, calls=%fused_computation.8 | custom fusion | bytes 8388736 | tf_op jit(solution)/shard_map/gather | solution.py:177
  157.5 3.0 %gather_fusion.7 = f32[32,64,512]{2,1,0:T(8,128)} fusion(f32[8,64,512]{2,1,0:T(8,128)S(1)} %squeeze.64, s32[1024]{0:T(1024)} %get-tuple-element.59), kind=kCustom, calls=%fused_computation.7 | custom fusion | bytes 8388736 | tf_op jit(solution)/shard_map/gather | solution.py:177
  160.4 6.3 %add_convert_fusion = bf16[32,64,512]{2,1,0:T(8,128)(2,1)} fusion(f32[32,64,512]{2,1,0:T(8,128)} %gather_fusion.8, f32[32,64,512]{2,1,0:T(8,128)} %gather_fusion.7, pred[32]{0:T(512)(128)(4,1)S(1)} %copy-done.27, pred[32]{0:T(512)(128)(4,1)S(1)} %copy-done.26), kind=kLoop, calls=%fused_computation.9 | loop fusion | flops 4194304 | bytes 10485824 | tf_op jit(solution)/shard_map/convert_element_type | solution.py:181
  166.7 16.2 %all-to-all-done.3 = bf16[32,64,512]{2,1,0:T(8,128)(2,1)} async-done(((bf16[32,64,512]{2,1,0:T(8,128)(2,1)}), bf16[32,64,512]{2,1,0:T(8,128)(2,1)}, u32[]{:S(2)}, u32[]{:S(2)}) %all-to-all-start.3) | async-done | bytes 2097184 | tf_op jit(solution)/shard_map/all_to_all | solution.py:184
  182.9 7.1 %all-to-all-start.4 = ((bf16[32,64,512]{2,1,0:T(8,128)(2,1)}), bf16[32,64,512]{2,1,0:T(8,128)(2,1)S(1)}, u32[]{:S(2)}, u32[]{:S(2)}) async-start(bf16[32,64,512]{2,1,0:T(8,128)(2,1)} %add_convert_fusion), calls=%async_computation.4 | async-start | bytes 4194304 | tf_op jit(solution)/shard_map/all_to_all | solution.py:184
  208.4 2.8 %fusion.8 = f32[8,64,512]{2,0,1:T(8,128)S(1)} fusion(bf16[32,64,512]{2,1,0:T(8,128)(2,1)} %all-to-all-done.3, s32[32]{0:T(128)S(1)} %copy-done.30), kind=kOutput, calls=%fused_computation.29 | convolution fusion | flops 16777472 | bytes 3145856 | tf_op jit(solution)/shard_map/rj,rtx->jtx/dot_general | solution.py:187
  211.3 5.5 %collective-permute-start.1 = (f32[8,64,512]{2,0,1:T(8,128)S(1)}, f32[8,64,512]{2,0,1:T(8,128)}, u32[]{:S(2)}, u32[]{:S(2)}) collective-permute-start(f32[8,64,512]{2,0,1:T(8,128)S(1)} %fusion.8), channel_id=1, source_target_pairs={{0,256},{256,0},{1,257},{257,1},{2,258},{258,2},{3,259},{259,3},{4... | collective-permute-start | bytes 3145736 | tf_op jit(solution)/shard_map/ppermute | solution.py:190
  220.8 15.2 %all-to-all-done.4 = bf16[32,64,512]{2,1,0:T(8,128)(2,1)S(1)} async-done(((bf16[32,64,512]{2,1,0:T(8,128)(2,1)}), bf16[32,64,512]{2,1,0:T(8,128)(2,1)S(1)}, u32[]{:S(2)}, u32[]{:S(2)}) %all-to-all-start.4) | async-done | bytes 2097184 | tf_op jit(solution)/shard_map/all_to_all | solution.py:184
  237.2 7.1 %collective-permute-start.2 = (f32[8,64,512]{2,0,1:T(8,128)S(1)}, f32[8,64,512]{2,0,1:T(8,128)S(1)}, u32[]{:S(2)}, u32[]{:S(2)}) collective-permute-start(f32[8,64,512]{2,0,1:T(8,128)S(1)} %fusion.6), channel_id=1, source_target_pairs={{0,256},{256,0},{1,257},{257,1},{2,258},{258,2},{3,259},{259,3},{4... | collective-permute-start | bytes 3145736 | tf_op jit(solution)/shard_map/ppermute | solution.py:190
  248.5 2.1 copy.235
  (187 shorter events, 77.8 us)
Async XLA Ops:
  2.0 34.0 %copy-start.22 = (s32[2,8]{1,0:T(2,128)}, s32[2,8]{1,0:T(2,128)S(1)}, u32[]{:S(2)}) copy-start(s32[2,8]{1,0:T(2,128)S(1)} %get-tuple-element.49) | copy-start | bytes 196
  2.1 13.2 %copy-start.28 = (s32[32]{0:T(128)}, s32[32]{0:T(128)S(1)}, u32[]{:S(2)}) copy-start(s32[32]{0:T(128)S(1)} %get-tuple-element.17) | copy-start | bytes 388
  2.8 19.0 %all-to-all-start = ((s32[32,1,2]{2,1,0:T(1,128)}), s32[32,1,2]{2,1,0:T(1,128)S(1)}, u32[]{:S(2)}, u32[]{:S(2)}) async-start(s32[32,1,2]{2,1,0:T(1,128)} %copy.121), calls=%async_computation | async-start | bytes 32768 | tf_op jit(solution)/shard_map/all_to_all | solution.py:100
  21.9 2.5 %copy-start.32 = (s32[32,1,2]{0,2,1:T(2,128)}, s32[32,1,2]{0,2,1:T(2,128)S(1)}, u32[]{:S(2)}) copy-start(s32[32,1,2]{0,2,1:T(2,128)S(1)} %copy.122) | copy-start | bytes 772
  22.4 2.0 copy-start.25
  24.4 4.2 %copy-start.31 = (s32[1,1,2,8]{3,2,1,0:T(2,128)S(1)}, s32[1,1,2,8]{3,2,1,0:T(2,128)}, u32[]{:S(2)}) copy-start(s32[1,1,2,8]{3,2,1,0:T(2,128)} %param.9) | copy-start | bytes 196
  24.4 51.2 %all-to-all-start.1 = ((bf16[32,64,512]{2,1,0:T(8,128)(2,1)}), bf16[32,64,512]{2,1,0:T(8,128)(2,1)S(1)}, u32[]{:S(2)}, u32[]{:S(2)}) async-start(bf16[32,64,512]{2,1,0:T(8,128)(2,1)} %gather_fusion), calls=%async_computation.1 | async-start | bytes 4194304 | tf_op jit(solution)/shard_map/all_to_all | solution.py:129
  34.7 5.6 %copy-start.4 = (bf16[2,64,4,4,128]{4,3,2,1,0:T(4,128)(2,1)S(1)}, bf16[2,64,4,4,128]{4,3,2,1,0:T(4,128)(2,1)}, u32[]{:S(2)}) copy-start(bf16[2,64,4,4,128]{4,3,2,1,0:T(4,128)(2,1)} %reshape.477) | copy-start | bytes 1572868
  42.2 49.4 %copy-start.2 = (bf16[2,64,2,4,128]{4,3,2,1,0:T(4,128)(2,1)}, bf16[2,64,2,4,128]{4,3,2,1,0:T(4,128)(2,1)S(1)}, u32[]{:S(2)}) copy-start(bf16[2,64,2,4,128]{4,3,2,1,0:T(4,128)(2,1)S(1)} %get-tuple-element.37) | copy-start | bytes 786436
  44.3 38.7 %copy-start.29 = (s32[32]{0:T(128)S(1)}, s32[32]{0:T(128)}, u32[]{:S(2)}) copy-start(s32[32]{0:T(128)} %copy-done.28) | copy-start | bytes 388
  44.3 38.7 %copy-start.33 = (s32[32,1,2]{0,2,1:T(2,128)S(1)}, s32[32,1,2]{0,2,1:T(2,128)}, u32[]{:S(2)}) copy-start(s32[32,1,2]{0,2,1:T(2,128)} %copy-done.32) | copy-start | bytes 772
  44.4 39.5 %copy-start.23 = (s32[2,8]{1,0:T(2,128)S(1)}, s32[2,8]{1,0:T(2,128)}, u32[]{:S(2)}) copy-start(s32[2,8]{1,0:T(2,128)} %copy-done.22) | copy-start | bytes 196
  44.4 39.7 %copy-start.24 = (s32[512]{0:T(512)S(1)}, s32[512]{0:T(512)}, u32[]{:S(2)}) copy-start(s32[512]{0:T(512)} %lt.76) | copy-start | bytes 6148
  75.6 53.4 %all-to-all-start.2 = ((bf16[32,64,512]{2,1,0:T(8,128)(2,1)}), bf16[32,64,512]{2,1,0:T(8,128)(2,1)}, u32[]{:S(2)}, u32[]{:S(2)}) async-start(bf16[32,64,512]{2,1,0:T(8,128)(2,1)} %gather_fusion.3), calls=%async_computation.2 | async-start | bytes 4194304 | tf_op jit(solution)/shard_map/all_to_all | solution.py:129
  105.4 3.1 %copy-start.26 = (pred[32]{0:T(512)(128)(4,1)S(1)}, pred[32]{0:T(512)(128)(4,1)}, u32[]{:S(2)}) copy-start(pred[32]{0:T(512)(128)(4,1)} %get-tuple-element.50) | copy-start | bytes 100
  105.4 3.1 %copy-start.27 = (pred[32]{0:T(512)(128)(4,1)S(1)}, pred[32]{0:T(512)(128)(4,1)}, u32[]{:S(2)}) copy-start(pred[32]{0:T(512)(128)(4,1)} %get-tuple-element.51) | copy-start | bytes 100
  129.0 53.9 %all-to-all-start.3 = ((bf16[32,64,512]{2,1,0:T(8,128)(2,1)}), bf16[32,64,512]{2,1,0:T(8,128)(2,1)}, u32[]{:S(2)}, u32[]{:S(2)}) async-start(bf16[32,64,512]{2,1,0:T(8,128)(2,1)} %add_convert_fusion.1), calls=%async_computation.3 | async-start | bytes 4194304 | tf_op jit(solution)/shard_map/all_to_all | solution.py:184
  166.7 23.4 %copy-start.17 = (bf16[2,2,128,128]{3,2,0,1:T(8,128)(2,1)S(1)}, bf16[2,2,128,128]{3,2,0,1:T(8,128)(2,1)}, u32[]{:S(2)}) copy-start(bf16[2,2,128,128]{3,2,0,1:T(8,128)(2,1)} %copy-done.16) | copy-start | bytes 393220
  182.9 53.0 %all-to-all-start.4 = ((bf16[32,64,512]{2,1,0:T(8,128)(2,1)}), bf16[32,64,512]{2,1,0:T(8,128)(2,1)S(1)}, u32[]{:S(2)}, u32[]{:S(2)}) async-start(bf16[32,64,512]{2,1,0:T(8,128)(2,1)} %add_convert_fusion), calls=%async_computation.4 | async-start | bytes 4194304 | tf_op jit(solution)/shard_map/all_to_all | solution.py:184
  199.4 9.0 %copy-start.30 = (s32[32]{0:T(128)S(1)}, s32[32]{0:T(128)}, u32[]{:S(2)}) copy-start(s32[32]{0:T(128)} %get-tuple-element.44) | copy-start | bytes 388
  207.4 9.4 %copy-start.13 = (bf16[1,1,128,256]{3,2,1,0:T(8,128)(2,1)S(1)}, bf16[1,1,128,256]{3,2,1,0:T(8,128)(2,1)}, u32[]{:S(2)}) copy-start(bf16[1,1,128,256]{3,2,1,0:T(8,128)(2,1)} %copy.152) | copy-start | bytes 196612
  211.3 33.0 %collective-permute-start.1 = (f32[8,64,512]{2,0,1:T(8,128)S(1)}, f32[8,64,512]{2,0,1:T(8,128)}, u32[]{:S(2)}, u32[]{:S(2)}) collective-permute-start(f32[8,64,512]{2,0,1:T(8,128)S(1)} %fusion.8), channel_id=1, source_target_pairs={{0,256},{256,0},{1,257},{257,1},{2,258},{258,2},{3,259},{259,3},{4... | collective-permute-start | bytes 3145736 | tf_op jit(solution)/shard_map/ppermute | solution.py:190
  219.5 24.8 %collective-permute-start = (bf16[1,1,128,3072]{3,2,1,0:T(8,128)(2,1)}, bf16[1,1,128,3072]{3,2,1,0:T(8,128)(2,1)}, u32[]{:S(2)}, u32[]{:S(2)}) collective-permute-start(bf16[1,1,128,3072]{3,2,1,0:T(8,128)(2,1)} %constant_dynamic-update-slice_fusion), channel_id=1, source_target_pairs={{32,0},{64,32},{96,64},{128,96},{160,128},{192,160},{224,192},{33,... | collective-permute-start | bytes 2359304 | tf_op jit(solution)/shard_map/ppermute | solution.py:20
  237.2 9.4 %collective-permute-start.2 = (f32[8,64,512]{2,0,1:T(8,128)S(1)}, f32[8,64,512]{2,0,1:T(8,128)S(1)}, u32[]{:S(2)}, u32[]{:S(2)}) collective-permute-start(f32[8,64,512]{2,0,1:T(8,128)S(1)} %fusion.6), channel_id=1, source_target_pairs={{0,256},{256,0},{1,257},{257,1},{2,258},{258,2},{3,259},{259,3},{4... | collective-permute-start | bytes 3145736 | tf_op jit(solution)/shard_map/ppermute | solution.py:190
  (18 other events, 19.9 us)

commit v2 on v1

--- a/solution.py
+++ b/solution.py
@@ -55,11 +55,11 @@
         * inv_root
     )
     grad_key = (
-        jnp.einsum("bighn,bighd->gbnd", dscores, queries, preferred_element_type=jnp.float32)
+        jnp.einsum("bighn,bighd->bngd", dscores, queries, preferred_element_type=jnp.float32)
         * inv_root
     )
     grad_value = jnp.einsum(
-        "bighn,bighd->gbnd", prob_bf, grad_rows, preferred_element_type=jnp.float32
+        "bighn,bighd->bngd", prob_bf, grad_rows, preferred_element_type=jnp.float32
     )
     return (grad_query, grad_key, grad_value)
 
@@ -154,22 +154,15 @@
             (queries_chunk, key_rows, value_rows, grads_chunk, log_total, attended),
         )
         query_parts.append(grad_query.reshape(tokens, per_chunk * groups * DH))
-        key_parts.append(
-            jnp.transpose(jnp.sum(grad_key[:, :, memory_len:], axis=1), (1, 0, 2)).reshape(
-                tokens, span
-            )
-        )
-        value_parts.append(
-            jnp.transpose(jnp.sum(grad_value[:, :, memory_len:], axis=1), (1, 0, 2)).reshape(
-                tokens, span
-            )
-        )
-        entry_grads = jnp.stack(
-            [grad_key[:, :, :memory_len], grad_value[:, :, :memory_len]], axis=0
-        )
-        entry_grads = jnp.transpose(
-            entry_grads.reshape(2, per_chunk, qblocks * topk, BLK, DH), (2, 3, 0, 1, 4)
-        ).reshape(qblocks * topk, BLK, 2 * span)
+        key_parts.append(jnp.sum(grad_key[:, memory_len:], axis=0).reshape(tokens, span))
+        value_parts.append(jnp.sum(grad_value[:, memory_len:], axis=0).reshape(tokens, span))
+        entry_grads = jnp.concatenate(
+            [
+                grad_key[:, :memory_len].reshape(qblocks * topk, BLK, span),
+                grad_value[:, :memory_len].reshape(qblocks * topk, BLK, span),
+            ],
+            axis=-1,
+        )
         by_block = entry_grads.reshape(qblocks, topk, BLK, 2 * span)
         slot_grads = sum(
             jnp.where(

time: 256 us -> 252 us (0.984); the launches traced: 251 us -> 251 us
  waiting for transfers between devices: 74.9 us -> 86.4 us
  other arithmetic: 34.9 us -> 24.6 us
  local copies, waits for them, and re-layouts: 72.5 us -> 69.2 us
  starting transfers between devices: 50.6 us -> 53.8 us
    convert_element_type x2, other arithmetic: 21.8 us -> 12.1 us  [per_device(): slot_grads = sum((jnp.where(present[block][:, None, None], by_block[block...]
    reshape x0 -> x4, local copies, waits for them, and re-layouts: none -> 9.01 us  [the longest x2 6.1 us: per_device(): grad_key[:, :memory_len].reshape(qblocks * topk, BLK, span)]
    slice x4 -> x8, local copies, waits for them, and re-layouts: 0.28 us -> 6.42 us  [the longest x4 3.7 us: per_device(): grad_key[:, :memory_len].reshape(qblocks * topk, BLK, span)]
    squeeze x4 -> x0, local copies, waits for them, and re-layouts: 5.81 us -> none  [per_device(): by_block[block].at[key_slot[block]].get(mode='promise_in_bounds')]
    all_to_all x2, waiting for transfers between devices: 36.2 us -> 42 us  [per_device(): lax.all_to_all(payload, 'mem', split_axis=0, concat_axis=0, tiled=True)]
    all_to_all x2, waiting for transfers between devices: 31.4 us -> 37.1 us  [per_device(): lax.all_to_all(sent_grads[chunk], 'mem', split_axis=0, concat_axis=0, til...]
    concatenate x7, local copies, waits for them, and re-layouts: 7 us -> 1.42 us  [per_device(): jnp.concatenate(query_parts + key_parts + value_parts, axis=-1)]
    slice x2, local copies, waits for them, and re-layouts: 3.61 us -> 0.42 us  [per_device(): by_block[block].at[key_slot[block]].get(mode='promise_in_bounds')]
  transfers between devices with their start and end apart: 8 -> 8, of which waited for: 6 -> 6; matrix products, arithmetic and copies ran while one was open for 44% -> 38% of each run, Pallas kernels for 0% -> 0%
where the time goes in v2:
time: 252 us; the launch traced here: 251 us
  waiting for transfers between devices  86.4 us (34%)
  local copies, waits for them, and re-layouts  69.2 us (27%)
  starting transfers between devices  53.8 us (21%)
  other arithmetic  24.6 us (10%)
  matrix products  14.9 us (6%)
    all_to_all x2, waiting for transfers between devices, per_device(): lax.all_to_all(payload, 'mem', split_axis=0, concat_axis=0, tiled=True)  42 us
    all_to_all x2, waiting for transfers between devices, per_device(): lax.all_to_all(sent_grads[chunk], 'mem', split_axis=0, concat_axis=0, til...  37.1 us
    all_to_all x2, starting transfers between devices, per_device(): lax.all_to_all(sent_grads[chunk], 'mem', split_axis=0, concat_axis=0, til...  17 us
    ppermute x2, starting transfers between devices, per_device(): partner = lax.ppermute(owned, 'dp', [(0, 1), (1, 0)])  13.4 us
    unnamed x75, local copies, waits for them, and re-layouts  12.5 us
    convert_element_type x2, other arithmetic, per_device(): slot_grads = sum((jnp.where(present[block][:, None, None], by_block[block...  12.1 us
    gather x4, local copies, waits for them, and re-layouts, per_device(): by_block[block].at[key_slot[block]].get(mode='promise_in_bounds')  11.9 us
    all_to_all x2, starting transfers between devices, per_device(): lax.all_to_all(payload, 'mem', split_axis=0, concat_axis=0, tiled=True)  11.7 us
  transfers between devices with their start and end apart: 8, of which 6 were waited for; matrix products, arithmetic and copies ran while one was open for 38% of the time, Pallas kernels for 0%

profile of v2, /device:TPU:1, one launch (start us, length us, event | category | flops | bytes accessed | tf_op | source)
XLA Modules:
  0.0 251.0 jit_solution(3901103455785727421)
XLA Ops:
  3.3 10.5 %all-to-all-start = ((s32[32,1,2]{2,1,0:T(1,128)}), s32[32,1,2]{2,1,0:T(1,128)S(1)}, u32[]{:S(2)}, u32[]{:S(2)}) async-start(s32[32,1,2]{2,1,0:T(1,128)} %copy.89), calls=%async_computation | async-start | bytes 32768 | tf_op jit(solution)/shard_map/all_to_all | solution.py:100
  15.9 6.5 %all-to-all-done = s32[32,1,2]{2,1,0:T(1,128)S(1)} async-done(((s32[32,1,2]{2,1,0:T(1,128)}), s32[32,1,2]{2,1,0:T(1,128)S(1)}, u32[]{:S(2)}, u32[]{:S(2)}) %all-to-all-start) | async-done | bytes 288 | tf_op jit(solution)/shard_map/all_to_all | solution.py:100
  25.1 4.1 %all-to-all-start.1 = ((bf16[32,64,512]{2,1,0:T(8,128)(2,1)}), bf16[32,64,512]{2,1,0:T(8,128)(2,1)S(1)}, u32[]{:S(2)}, u32[]{:S(2)}) async-start(bf16[32,64,512]{2,1,0:T(8,128)(2,1)} %gather_fusion), calls=%async_computation.1 | async-start | bytes 4194304 | tf_op jit(solution)/shard_map/all_to_all | solution.py:129
  32.6 2.2 reshape_squeeze.3
  43.9 2.2 gather_fusion.3
  46.1 30.1 %all-to-all-done.1 = bf16[32,64,512]{2,1,0:T(8,128)(2,1)S(1)} async-done(((bf16[32,64,512]{2,1,0:T(8,128)(2,1)}), bf16[32,64,512]{2,1,0:T(8,128)(2,1)S(1)}, u32[]{:S(2)}, u32[]{:S(2)}) %all-to-all-start.1) | async-done | bytes 2097184 | tf_op jit(solution)/shard_map/all_to_all | solution.py:129
  76.2 7.6 %all-to-all-start.2 = ((bf16[32,64,512]{2,1,0:T(8,128)(2,1)}), bf16[32,64,512]{2,1,0:T(8,128)(2,1)}, u32[]{:S(2)}, u32[]{:S(2)}) async-start(bf16[32,64,512]{2,1,0:T(8,128)(2,1)} %gather_fusion.3), calls=%async_computation.2 | async-start | bytes 4194304 | tf_op jit(solution)/shard_map/all_to_all | solution.py:129
  95.9 3.0 %reshape.483 = f32[16,64,256]{2,1,0:T(8,128)} reshape(f32[2,512,2,128]{3,2,1,0:T(2,128)} %copy.98) | data formatting | bytes 2097152 | tf_op jit(solution)/shard_map/reshape | solution.py:161
  105.4 3.0 %gather_fusion.4 = f32[32,64,512]{2,1,0:T(8,128)} fusion(f32[8,64,512]{2,1,0:T(8,128)S(1)} %get-tuple-element.20, s32[1024]{0:T(1024)} %get-tuple-element.59), kind=kCustom, calls=%fused_computation.4 | custom fusion | bytes 8388736 | tf_op jit(solution)/shard_map/gather | solution.py:170
  108.3 3.0 %gather_fusion.5 = f32[32,64,512]{2,1,0:T(8,128)} fusion(f32[8,64,512]{2,1,0:T(8,128)S(1)} %get-tuple-element.21, s32[1024]{0:T(1024)} %get-tuple-element.58), kind=kCustom, calls=%fused_computation.5 | custom fusion | bytes 8388736 | tf_op jit(solution)/shard_map/gather | solution.py:170
  111.4 6.1 %add_convert_fusion.1 = bf16[32,64,512]{2,1,0:T(8,128)(2,1)} fusion(f32[32,64,512]{2,1,0:T(8,128)} %gather_fusion.5, f32[32,64,512]{2,1,0:T(8,128)} %gather_fusion.4, pred[32]{0:T(512)(128)(4,1)S(1)} %copy-done.23, pred[32]{0:T(512)(128)(4,1)S(1)} %copy-done.22), kind=kLoop, calls=%fused_computation.10 | loop fusion | flops 4194304 | bytes 10485824 | tf_op jit(solution)/shard_map/convert_element_type | solution.py:174
  117.4 11.8 %all-to-all-done.2 = bf16[32,64,512]{2,1,0:T(8,128)(2,1)} async-done(((bf16[32,64,512]{2,1,0:T(8,128)(2,1)}), bf16[32,64,512]{2,1,0:T(8,128)(2,1)}, u32[]{:S(2)}, u32[]{:S(2)}) %all-to-all-start.2) | async-done | bytes 2097184 | tf_op jit(solution)/shard_map/all_to_all | solution.py:129
  129.3 8.2 %all-to-all-start.3 = ((bf16[32,64,512]{2,1,0:T(8,128)(2,1)}), bf16[32,64,512]{2,1,0:T(8,128)(2,1)}, u32[]{:S(2)}, u32[]{:S(2)}) async-start(bf16[32,64,512]{2,1,0:T(8,128)(2,1)} %add_convert_fusion.1), calls=%async_computation.3 | async-start | bytes 4194304 | tf_op jit(solution)/shard_map/all_to_all | solution.py:177
  137.5 2.2 gather_fusion.6
  147.6 3.1 %reshape.486 = f32[16,64,256]{2,1,0:T(8,128)} reshape(f32[2,512,2,128]{3,2,1,0:T(2,128)} %copy.116) | data formatting | bytes 2097152 | tf_op jit(solution)/shard_map/reshape | solution.py:161
  154.9 2.9 %gather_fusion.7 = f32[32,64,512]{2,1,0:T(8,128)} fusion(f32[8,64,512]{2,1,0:T(8,128)S(1)} %get-tuple-element.18, s32[1024]{0:T(1024)} %get-tuple-element.59), kind=kCustom, calls=%fused_computation.7 | custom fusion | bytes 8388736 | tf_op jit(solution)/shard_map/gather | solution.py:170
  157.8 3.0 %gather_fusion.8 = f32[32,64,512]{2,1,0:T(8,128)} fusion(f32[8,64,512]{2,1,0:T(8,128)S(1)} %get-tuple-element.19, s32[1024]{0:T(1024)} %get-tuple-element.58), kind=kCustom, calls=%fused_computation.8 | custom fusion | bytes 8388736 | tf_op jit(solution)/shard_map/gather | solution.py:170
  160.7 6.0 %add_convert_fusion = bf16[32,64,512]{2,1,0:T(8,128)(2,1)} fusion(f32[32,64,512]{2,1,0:T(8,128)} %gather_fusion.8, f32[32,64,512]{2,1,0:T(8,128)} %gather_fusion.7, pred[32]{0:T(512)(128)(4,1)S(1)} %copy-done.23, pred[32]{0:T(512)(128)(4,1)S(1)} %copy-done.22), kind=kLoop, calls=%fused_computation.9 | loop fusion | flops 4194304 | bytes 10485824 | tf_op jit(solution)/shard_map/convert_element_type | solution.py:174
  166.8 15.3 %all-to-all-done.3 = bf16[32,64,512]{2,1,0:T(8,128)(2,1)} async-done(((bf16[32,64,512]{2,1,0:T(8,128)(2,1)}), bf16[32,64,512]{2,1,0:T(8,128)(2,1)}, u32[]{:S(2)}, u32[]{:S(2)}) %all-to-all-start.3) | async-done | bytes 2097184 | tf_op jit(solution)/shard_map/all_to_all | solution.py:177
  182.1 8.8 %all-to-all-start.4 = ((bf16[32,64,512]{2,1,0:T(8,128)(2,1)}), bf16[32,64,512]{2,1,0:T(8,128)(2,1)S(1)}, u32[]{:S(2)}, u32[]{:S(2)}) async-start(bf16[32,64,512]{2,1,0:T(8,128)(2,1)} %add_convert_fusion), calls=%async_computation.4 | async-start | bytes 4194304 | tf_op jit(solution)/shard_map/all_to_all | solution.py:177
  201.8 2.8 %fusion.8 = f32[8,64,512]{2,0,1:T(8,128)S(1)} fusion(bf16[32,64,512]{2,1,0:T(8,128)(2,1)} %all-to-all-done.3, s32[32]{0:T(128)S(1)} %copy-done.27), kind=kOutput, calls=%fused_computation.27 | convolution fusion | flops 16777472 | bytes 3145856 | tf_op jit(solution)/shard_map/rj,rtx->jtx/dot_general | solution.py:180
  204.6 5.5 %collective-permute-start.1 = (f32[8,64,512]{2,0,1:T(8,128)S(1)}, f32[8,64,512]{2,0,1:T(8,128)}, u32[]{:S(2)}, u32[]{:S(2)}) collective-permute-start(f32[8,64,512]{2,0,1:T(8,128)S(1)} %fusion.8), channel_id=1, source_target_pairs={{0,256},{256,0},{1,257},{257,1},{2,258},{258,2},{3,259},{259,3},{4... | collective-permute-start | bytes 3145736 | tf_op jit(solution)/shard_map/ppermute | solution.py:183
  213.8 21.8 %all-to-all-done.4 = bf16[32,64,512]{2,1,0:T(8,128)(2,1)S(1)} async-done(((bf16[32,64,512]{2,1,0:T(8,128)(2,1)}), bf16[32,64,512]{2,1,0:T(8,128)(2,1)S(1)}, u32[]{:S(2)}, u32[]{:S(2)}) %all-to-all-start.4) | async-done | bytes 2097184 | tf_op jit(solution)/shard_map/all_to_all | solution.py:177
  236.8 7.8 %collective-permute-start.2 = (f32[8,64,512]{2,0,1:T(8,128)S(1)}, f32[8,64,512]{2,0,1:T(8,128)S(1)}, u32[]{:S(2)}, u32[]{:S(2)}) collective-permute-start(f32[8,64,512]{2,0,1:T(8,128)S(1)} %fusion.6), channel_id=1, source_target_pairs={{0,256},{256,0},{1,257},{257,1},{2,258},{258,2},{3,259},{259,3},{4... | collective-permute-start | bytes 3145736 | tf_op jit(solution)/shard_map/ppermute | solution.py:183
  (185 shorter events, 71.3 us)
Async XLA Ops:
  2.6 13.2 %copy-start.25 = (s32[32]{0:T(128)}, s32[32]{0:T(128)S(1)}, u32[]{:S(2)}) copy-start(s32[32]{0:T(128)S(1)} %get-tuple-element.17) | copy-start | bytes 388
  3.3 19.0 %all-to-all-start = ((s32[32,1,2]{2,1,0:T(1,128)}), s32[32,1,2]{2,1,0:T(1,128)S(1)}, u32[]{:S(2)}, u32[]{:S(2)}) async-start(s32[32,1,2]{2,1,0:T(1,128)} %copy.89), calls=%async_computation | async-start | bytes 32768 | tf_op jit(solution)/shard_map/all_to_all | solution.py:100
  23.0 2.0 copy-start.21
  25.1 4.2 %copy-start.28 = (s32[1,1,2,8]{3,2,1,0:T(2,128)S(1)}, s32[1,1,2,8]{3,2,1,0:T(2,128)}, u32[]{:S(2)}) copy-start(s32[1,1,2,8]{3,2,1,0:T(2,128)} %param.9) | copy-start | bytes 196
  25.1 51.2 %all-to-all-start.1 = ((bf16[32,64,512]{2,1,0:T(8,128)(2,1)}), bf16[32,64,512]{2,1,0:T(8,128)(2,1)S(1)}, u32[]{:S(2)}, u32[]{:S(2)}) async-start(bf16[32,64,512]{2,1,0:T(8,128)(2,1)} %gather_fusion), calls=%async_computation.1 | async-start | bytes 4194304 | tf_op jit(solution)/shard_map/all_to_all | solution.py:129
  29.4 5.4 %copy-start.24 = (s32[2,32]{1,0:T(2,128)S(1)}, s32[2,32]{1,0:T(2,128)}, u32[]{:S(2)}) copy-start(s32[2,32]{1,0:T(2,128)} %get-tuple-element.16) | copy-start | bytes 772
  34.7 6.5 %copy-start.9 = (bf16[2,64,4,4,128]{4,3,2,1,0:T(4,128)(2,1)S(1)}, bf16[2,64,4,4,128]{4,3,2,1,0:T(4,128)(2,1)}, u32[]{:S(2)}) copy-start(bf16[2,64,4,4,128]{4,3,2,1,0:T(4,128)(2,1)} %reshape_squeeze.3) | copy-start | bytes 1572868
  35.5 5.9 %copy-start.26 = (s32[32]{0:T(128)S(1)}, s32[32]{0:T(128)}, u32[]{:S(2)}) copy-start(s32[32]{0:T(128)} %copy-done.25) | copy-start | bytes 388
  35.5 5.9 %copy-start.30 = (s32[32,1,2]{0,2,1:T(2,128)S(1)}, s32[32,1,2]{0,2,1:T(2,128)}, u32[]{:S(2)}) copy-start(s32[32,1,2]{0,2,1:T(2,128)} %copy-done.29) | copy-start | bytes 772
  46.1 37.7 %copy-start.31 = (s32[2,8]{1,0:T(2,128)S(1)}, s32[2,8]{1,0:T(2,128)}, u32[]{:S(2)}) copy-start(s32[2,8]{1,0:T(2,128)} %gather.33) | copy-start | bytes 196
  46.1 37.9 %copy-start.20 = (pred[2,64,128]{2,1,0:T(8,128)(4,1)S(1)}, pred[2,64,128]{2,1,0:T(8,128)(4,1)}, u32[]{:S(2)}) copy-start(pred[2,64,128]{2,1,0:T(8,128)(4,1)} %iota_compare_fusion) | copy-start | bytes 49156
  76.2 53.0 %all-to-all-start.2 = ((bf16[32,64,512]{2,1,0:T(8,128)(2,1)}), bf16[32,64,512]{2,1,0:T(8,128)(2,1)}, u32[]{:S(2)}, u32[]{:S(2)}) async-start(bf16[32,64,512]{2,1,0:T(8,128)(2,1)} %gather_fusion.3), calls=%async_computation.2 | async-start | bytes 4194304 | tf_op jit(solution)/shard_map/all_to_all | solution.py:129
  92.3 1.8 copy-start.4
  101.0 3.9 %copy-start.7 = (f32[16,64,256]{2,1,0:T(8,128)S(1)}, f32[16,64,256]{2,1,0:T(8,128)}, u32[]{:S(2)}) copy-start(f32[16,64,256]{2,1,0:T(8,128)} %reshape.483) | copy-start | bytes 3145732
  108.3 3.0 %copy-start.22 = (pred[32]{0:T(512)(128)(4,1)S(1)}, pred[32]{0:T(512)(128)(4,1)}, u32[]{:S(2)}) copy-start(pred[32]{0:T(512)(128)(4,1)} %get-tuple-element.50) | copy-start | bytes 100
  108.3 3.0 %copy-start.23 = (pred[32]{0:T(512)(128)(4,1)S(1)}, pred[32]{0:T(512)(128)(4,1)}, u32[]{:S(2)}) copy-start(pred[32]{0:T(512)(128)(4,1)} %get-tuple-element.51) | copy-start | bytes 100
  129.3 52.8 %all-to-all-start.3 = ((bf16[32,64,512]{2,1,0:T(8,128)(2,1)}), bf16[32,64,512]{2,1,0:T(8,128)(2,1)}, u32[]{:S(2)}, u32[]{:S(2)}) async-start(bf16[32,64,512]{2,1,0:T(8,128)(2,1)} %add_convert_fusion.1), calls=%async_computation.3 | async-start | bytes 4194304 | tf_op jit(solution)/shard_map/all_to_all | solution.py:177
  166.8 24.1 %copy-start.5 = (bf16[2,64,2,4,640]{4,1,3,2,0:T(8,128)(2,1)S(1)}, bf16[2,64,2,4,640]{4,1,3,2,0:T(8,128)(2,1)}, u32[]{:S(2)}) copy-start(bf16[2,64,2,4,640]{4,1,3,2,0:T(8,128)(2,1)} %copy-done.4) | copy-start | bytes 3932164
  166.8 24.1 %copy-start.16 = (bf16[2,2,128,128]{3,2,0,1:T(8,128)(2,1)S(1)}, bf16[2,2,128,128]{3,2,0,1:T(8,128)(2,1)}, u32[]{:S(2)}) copy-start(bf16[2,2,128,128]{3,2,0,1:T(8,128)(2,1)} %copy-done.15) | copy-start | bytes 393220
  182.1 53.5 %all-to-all-start.4 = ((bf16[32,64,512]{2,1,0:T(8,128)(2,1)}), bf16[32,64,512]{2,1,0:T(8,128)(2,1)S(1)}, u32[]{:S(2)}, u32[]{:S(2)}) async-start(bf16[32,64,512]{2,1,0:T(8,128)(2,1)} %add_convert_fusion), calls=%async_computation.4 | async-start | bytes 4194304 | tf_op jit(solution)/shard_map/all_to_all | solution.py:177
  196.1 5.6 %copy-start.27 = (s32[32]{0:T(128)S(1)}, s32[32]{0:T(128)}, u32[]{:S(2)}) copy-start(s32[32]{0:T(128)} %get-tuple-element.44) | copy-start | bytes 388
  204.6 40.1 %collective-permute-start.1 = (f32[8,64,512]{2,0,1:T(8,128)S(1)}, f32[8,64,512]{2,0,1:T(8,128)}, u32[]{:S(2)}, u32[]{:S(2)}) collective-permute-start(f32[8,64,512]{2,0,1:T(8,128)S(1)} %fusion.8), channel_id=1, source_target_pairs={{0,256},{256,0},{1,257},{257,1},{2,258},{258,2},{3,259},{259,3},{4... | collective-permute-start | bytes 3145736 | tf_op jit(solution)/shard_map/ppermute | solution.py:183
  212.5 32.1 %collective-permute-start = (bf16[1,1,128,3072]{3,2,1,0:T(8,128)(2,1)}, bf16[1,1,128,3072]{3,2,1,0:T(8,128)(2,1)}, u32[]{:S(2)}, u32[]{:S(2)}) collective-permute-start(bf16[1,1,128,3072]{3,2,1,0:T(8,128)(2,1)} %constant_dynamic-update-slice_fusion.2), channel_id=1, source_target_pairs={{32,0},{64,32},{96,64},{128,96},{160,128},{192,160},{224,192},{33,... | collective-permute-start | bytes 2359304 | tf_op jit(solution)/shard_map/ppermute | solution.py:20
  236.8 10.1 %collective-permute-start.2 = (f32[8,64,512]{2,0,1:T(8,128)S(1)}, f32[8,64,512]{2,0,1:T(8,128)S(1)}, u32[]{:S(2)}, u32[]{:S(2)}) collective-permute-start(f32[8,64,512]{2,0,1:T(8,128)S(1)} %fusion.6), channel_id=1, source_target_pairs={{0,256},{256,0},{1,257},{257,1},{2,258},{258,2},{3,259},{259,3},{4... | collective-permute-start | bytes 3145736 | tf_op jit(solution)/shard_map/ppermute | solution.py:183
  (16 other events, 19.1 us)

commit v3 on v2

--- a/solution.py
+++ b/solution.py
@@ -185,7 +185,12 @@
     section_grads = jnp.concatenate(query_parts + key_parts + value_parts, axis=-1).astype(
         jnp.bfloat16
     )
-    upstream = passed_along(section_grads[None, None], "section", -1)
+    sections = lax.axis_size("section")
+    cycled = lax.ppermute(
+        section_grads, "section", [(i, (i - 1) % sections) for i in range(sections)]
+    )
+    last = lax.axis_index("section") == sections - 1
+    upstream = jnp.where(last, jnp.zeros_like(cycled), cycled)[None, None]
     summed = jnp.concatenate(
         [part[:, :, :span] for part in owned_parts] + [part[:, :, span:] for part in owned_parts],
         axis=-1,

time: 252 us -> 252 us (level)
  waiting for transfers between devices: 86.4 us -> 71.1 us
  starting transfers between devices: 53.8 us -> 63.4 us
  local copies, waits for them, and re-layouts: 69.2 us -> 72.3 us
    all_to_all x2, waiting for transfers between devices: 37.1 us -> 22.6 us  [per_device(): lax.all_to_all(sent_grads[chunk], 'mem', split_axis=0, concat_axis=0, til...]
    ppermute x1, starting transfers between devices: 1.28 us -> 10.7 us  [per_device(): lax.ppermute(section_grads, 'section', [(i, (i - 1) % sections) for i in...]
    reshape x0 -> x6, local copies, waits for them, and re-layouts: none -> 4.08 us  [the longest x2 1.99 us: per_device(): query_parts.append(grad_query.reshape(tokens, per_chunk * groups * DH))]
    unnamed x75 -> x78, local copies, waits for them, and re-layouts: 12.5 us -> 10.4 us
  transfers between devices with their start and end apart: 8 -> 8, of which waited for: 6 -> 5; matrix products, arithmetic and copies ran while one was open for 38% -> 41% of each run, Pallas kernels for 0% -> 0%
where the time goes in v3:
time: 252 us; the launch traced here: 250 us
  local copies, waits for them, and re-layouts  72.3 us (29%)
  waiting for transfers between devices  71.1 us (28%)
  starting transfers between devices  63.4 us (25%)
  other arithmetic  26.8 us (11%)
  matrix products  14.5 us (6%)
    all_to_all x2, waiting for transfers between devices, per_device(): lax.all_to_all(payload, 'mem', split_axis=0, concat_axis=0, tiled=True)  42 us
    all_to_all x2, waiting for transfers between devices, per_device(): lax.all_to_all(sent_grads[chunk], 'mem', split_axis=0, concat_axis=0, til...  22.6 us
    all_to_all x2, starting transfers between devices, per_device(): lax.all_to_all(sent_grads[chunk], 'mem', split_axis=0, concat_axis=0, til...  17 us
    ppermute x2, starting transfers between devices, per_device(): partner = lax.ppermute(owned, 'dp', [(0, 1), (1, 0)])  13.6 us
    convert_element_type x2, other arithmetic, per_device(): slot_grads = sum((jnp.where(present[block][:, None, None], by_block[block...  12.1 us
    gather x4, local copies, waits for them, and re-layouts, per_device(): by_block[block].at[key_slot[block]].get(mode='promise_in_bounds')  11.8 us
    all_to_all x2, starting transfers between devices, per_device(): lax.all_to_all(payload, 'mem', split_axis=0, concat_axis=0, tiled=True)  11.7 us
    ppermute x1, starting transfers between devices, per_device(): lax.ppermute(section_grads, 'section', [(i, (i - 1) % sections) for i in...  10.7 us
  transfers between devices with their start and end apart: 8, of which 5 were waited for; matrix products, arithmetic and copies ran while one was open for 41% of the time, Pallas kernels for 0%

profile of v3, /device:TPU:1, one launch (start us, length us, event | category | flops | bytes accessed | tf_op | source)
XLA Modules:
  0.0 250.2 jit_solution(17465274239459316122)
XLA Ops:
  3.3 10.5 %all-to-all-start = ((s32[32,1,2]{2,1,0:T(1,128)}), s32[32,1,2]{2,1,0:T(1,128)S(1)}, u32[]{:S(2)}, u32[]{:S(2)}) async-start(s32[32,1,2]{2,1,0:T(1,128)} %copy.89), calls=%async_computation | async-start | bytes 32768 | tf_op jit(solution)/shard_map/all_to_all | solution.py:100
  15.9 6.5 %all-to-all-done = s32[32,1,2]{2,1,0:T(1,128)S(1)} async-done(((s32[32,1,2]{2,1,0:T(1,128)}), s32[32,1,2]{2,1,0:T(1,128)S(1)}, u32[]{:S(2)}, u32[]{:S(2)}) %all-to-all-start) | async-done | bytes 288 | tf_op jit(solution)/shard_map/all_to_all | solution.py:100
  25.1 4.1 %all-to-all-start.1 = ((bf16[32,64,512]{2,1,0:T(8,128)(2,1)}), bf16[32,64,512]{2,1,0:T(8,128)(2,1)S(1)}, u32[]{:S(2)}, u32[]{:S(2)}) async-start(bf16[32,64,512]{2,1,0:T(8,128)(2,1)} %gather_fusion), calls=%async_computation.1 | async-start | bytes 4194304 | tf_op jit(solution)/shard_map/all_to_all | solution.py:129
  32.6 2.2 reshape_squeeze.3
  46.1 30.2 %all-to-all-done.1 = bf16[32,64,512]{2,1,0:T(8,128)(2,1)S(1)} async-done(((bf16[32,64,512]{2,1,0:T(8,128)(2,1)}), bf16[32,64,512]{2,1,0:T(8,128)(2,1)S(1)}, u32[]{:S(2)}, u32[]{:S(2)}) %all-to-all-start.1) | async-done | bytes 2097184 | tf_op jit(solution)/shard_map/all_to_all | solution.py:129
  76.3 7.6 %all-to-all-start.2 = ((bf16[32,64,512]{2,1,0:T(8,128)(2,1)}), bf16[32,64,512]{2,1,0:T(8,128)(2,1)}, u32[]{:S(2)}, u32[]{:S(2)}) async-start(bf16[32,64,512]{2,1,0:T(8,128)(2,1)} %gather_fusion.3), calls=%async_computation.2 | async-start | bytes 4194304 | tf_op jit(solution)/shard_map/all_to_all | solution.py:129
  95.9 3.0 %reshape.409 = f32[16,64,256]{2,1,0:T(8,128)} reshape(f32[2,512,2,128]{3,2,1,0:T(2,128)} %copy.98) | data formatting | bytes 2097152 | tf_op jit(solution)/shard_map/reshape | solution.py:161
  105.4 3.0 %gather_fusion.4 = f32[32,64,512]{2,1,0:T(8,128)} fusion(f32[8,64,512]{2,1,0:T(8,128)S(1)} %get-tuple-element.20, s32[1024]{0:T(1024)} %get-tuple-element.59), kind=kCustom, calls=%fused_computation.4 | custom fusion | bytes 8388736 | tf_op jit(solution)/shard_map/gather | solution.py:170
  108.4 3.0 %gather_fusion.5 = f32[32,64,512]{2,1,0:T(8,128)} fusion(f32[8,64,512]{2,1,0:T(8,128)S(1)} %get-tuple-element.21, s32[1024]{0:T(1024)} %get-tuple-element.58), kind=kCustom, calls=%fused_computation.5 | custom fusion | bytes 8388736 | tf_op jit(solution)/shard_map/gather | solution.py:170
  111.4 6.1 %add_convert_fusion.1 = bf16[32,64,512]{2,1,0:T(8,128)(2,1)} fusion(f32[32,64,512]{2,1,0:T(8,128)} %gather_fusion.5, f32[32,64,512]{2,1,0:T(8,128)} %gather_fusion.4, pred[32]{0:T(512)(128)(4,1)S(1)} %copy-done.25, pred[32]{0:T(512)(128)(4,1)S(1)} %copy-done.24), kind=kLoop, calls=%fused_computation.10 | loop fusion | flops 4194304 | bytes 10485824 | tf_op jit(solution)/shard_map/convert_element_type | solution.py:174
  117.5 11.8 %all-to-all-done.2 = bf16[32,64,512]{2,1,0:T(8,128)(2,1)} async-done(((bf16[32,64,512]{2,1,0:T(8,128)(2,1)}), bf16[32,64,512]{2,1,0:T(8,128)(2,1)}, u32[]{:S(2)}, u32[]{:S(2)}) %all-to-all-start.2) | async-done | bytes 2097184 | tf_op jit(solution)/shard_map/all_to_all | solution.py:129
  129.3 8.2 %all-to-all-start.3 = ((bf16[32,64,512]{2,1,0:T(8,128)(2,1)}), bf16[32,64,512]{2,1,0:T(8,128)(2,1)}, u32[]{:S(2)}, u32[]{:S(2)}) async-start(bf16[32,64,512]{2,1,0:T(8,128)(2,1)} %add_convert_fusion.1), calls=%async_computation.3 | async-start | bytes 4194304 | tf_op jit(solution)/shard_map/all_to_all | solution.py:177
  137.5 2.2 gather_fusion.6
  147.6 3.1 %reshape.417 = f32[16,64,256]{2,1,0:T(8,128)} reshape(f32[2,512,2,128]{3,2,1,0:T(2,128)} %copy.116) | data formatting | bytes 2097152 | tf_op jit(solution)/shard_map/reshape | solution.py:161
  154.9 2.9 %gather_fusion.7 = f32[32,64,512]{2,1,0:T(8,128)} fusion(f32[8,64,512]{2,1,0:T(8,128)S(1)} %get-tuple-element.18, s32[1024]{0:T(1024)} %get-tuple-element.59), kind=kCustom, calls=%fused_computation.7 | custom fusion | bytes 8388736 | tf_op jit(solution)/shard_map/gather | solution.py:170
  157.8 3.0 %gather_fusion.8 = f32[32,64,512]{2,1,0:T(8,128)} fusion(f32[8,64,512]{2,1,0:T(8,128)S(1)} %get-tuple-element.19, s32[1024]{0:T(1024)} %get-tuple-element.58), kind=kCustom, calls=%fused_computation.8 | custom fusion | bytes 8388736 | tf_op jit(solution)/shard_map/gather | solution.py:170
  160.8 6.0 %add_convert_fusion = bf16[32,64,512]{2,1,0:T(8,128)(2,1)} fusion(f32[32,64,512]{2,1,0:T(8,128)} %gather_fusion.8, f32[32,64,512]{2,1,0:T(8,128)} %gather_fusion.7, pred[32]{0:T(512)(128)(4,1)S(1)} %copy-done.25, pred[32]{0:T(512)(128)(4,1)S(1)} %copy-done.24), kind=kLoop, calls=%fused_computation.9 | loop fusion | flops 4194304 | bytes 10485824 | tf_op jit(solution)/shard_map/convert_element_type | solution.py:174
  166.8 15.3 %all-to-all-done.3 = bf16[32,64,512]{2,1,0:T(8,128)(2,1)} async-done(((bf16[32,64,512]{2,1,0:T(8,128)(2,1)}), bf16[32,64,512]{2,1,0:T(8,128)(2,1)}, u32[]{:S(2)}, u32[]{:S(2)}) %all-to-all-start.3) | async-done | bytes 2097184 | tf_op jit(solution)/shard_map/all_to_all | solution.py:177
  182.2 8.8 %all-to-all-start.4 = ((bf16[32,64,512]{2,1,0:T(8,128)(2,1)}), bf16[32,64,512]{2,1,0:T(8,128)(2,1)S(1)}, u32[]{:S(2)}, u32[]{:S(2)}) async-start(bf16[32,64,512]{2,1,0:T(8,128)(2,1)} %add_convert_fusion), calls=%async_computation.4 | async-start | bytes 4194304 | tf_op jit(solution)/shard_map/all_to_all | solution.py:177
  209.0 10.7 %collective-permute-start = (bf16[128,3072]{1,0:T(8,128)(2,1)}, bf16[128,3072]{1,0:T(8,128)(2,1)}, u32[]{:S(2)}, u32[]{:S(2)}) collective-permute-start(bf16[128,3072]{1,0:T(8,128)(2,1)} %constant_dynamic-update-slice_fusion.2), channel_id=1, source_target_pairs={{0,224},{32,0},{64,32},{96,64},{128,96},{160,128},{192,160},{224,1... | collective-permute-start | bytes 2359304 | tf_op jit(solution)/shard_map/ppermute | solution.py:189
  219.7 2.8 %fusion.8 = f32[8,64,512]{2,0,1:T(8,128)S(1)} fusion(bf16[32,64,512]{2,1,0:T(8,128)(2,1)} %all-to-all-done.3, s32[32]{0:T(128)S(1)} %copy-done.29), kind=kOutput, calls=%fused_computation.27 | convolution fusion | flops 16777472 | bytes 3145856 | tf_op jit(solution)/shard_map/rj,rtx->jtx/dot_general | solution.py:180
  222.5 5.8 %collective-permute-start.1 = (f32[8,64,512]{2,0,1:T(8,128)S(1)}, f32[8,64,512]{2,0,1:T(8,128)}, u32[]{:S(2)}, u32[]{:S(2)}) collective-permute-start(f32[8,64,512]{2,0,1:T(8,128)S(1)} %fusion.8), channel_id=1, source_target_pairs={{0,256},{256,0},{1,257},{257,1},{2,258},{258,2},{3,259},{259,3},{4... | collective-permute-start | bytes 3145736 | tf_op jit(solution)/shard_map/ppermute | solution.py:183
  228.4 7.3 %all-to-all-done.4 = bf16[32,64,512]{2,1,0:T(8,128)(2,1)S(1)} async-done(((bf16[32,64,512]{2,1,0:T(8,128)(2,1)}), bf16[32,64,512]{2,1,0:T(8,128)(2,1)S(1)}, u32[]{:S(2)}, u32[]{:S(2)}) %all-to-all-start.4) | async-done | bytes 2097184 | tf_op jit(solution)/shard_map/all_to_all | solution.py:177
  236.9 7.8 %collective-permute-start.2 = (f32[8,64,512]{2,0,1:T(8,128)S(1)}, f32[8,64,512]{2,0,1:T(8,128)S(1)}, u32[]{:S(2)}, u32[]{:S(2)}) collective-permute-start(f32[8,64,512]{2,0,1:T(8,128)S(1)} %fusion.6), channel_id=1, source_target_pairs={{0,256},{256,0},{1,257},{257,1},{2,258},{258,2},{3,259},{259,3},{4... | collective-permute-start | bytes 3145736 | tf_op jit(solution)/shard_map/ppermute | solution.py:183
  (189 shorter events, 76.3 us)
Async XLA Ops:
  2.6 13.2 %copy-start.27 = (s32[32]{0:T(128)}, s32[32]{0:T(128)S(1)}, u32[]{:S(2)}) copy-start(s32[32]{0:T(128)S(1)} %get-tuple-element.17) | copy-start | bytes 388
  3.3 19.0 %all-to-all-start = ((s32[32,1,2]{2,1,0:T(1,128)}), s32[32,1,2]{2,1,0:T(1,128)S(1)}, u32[]{:S(2)}, u32[]{:S(2)}) async-start(s32[32,1,2]{2,1,0:T(1,128)} %copy.89), calls=%async_computation | async-start | bytes 32768 | tf_op jit(solution)/shard_map/all_to_all | solution.py:100
  25.1 4.2 %copy-start.30 = (s32[1,1,2,8]{3,2,1,0:T(2,128)S(1)}, s32[1,1,2,8]{3,2,1,0:T(2,128)}, u32[]{:S(2)}) copy-start(s32[1,1,2,8]{3,2,1,0:T(2,128)} %param.9) | copy-start | bytes 196
  25.1 51.2 %all-to-all-start.1 = ((bf16[32,64,512]{2,1,0:T(8,128)(2,1)}), bf16[32,64,512]{2,1,0:T(8,128)(2,1)S(1)}, u32[]{:S(2)}, u32[]{:S(2)}) async-start(bf16[32,64,512]{2,1,0:T(8,128)(2,1)} %gather_fusion), calls=%async_computation.1 | async-start | bytes 4194304 | tf_op jit(solution)/shard_map/all_to_all | solution.py:129
  29.4 5.4 %copy-start.26 = (s32[2,32]{1,0:T(2,128)S(1)}, s32[2,32]{1,0:T(2,128)}, u32[]{:S(2)}) copy-start(s32[2,32]{1,0:T(2,128)} %get-tuple-element.16) | copy-start | bytes 772
  34.8 6.4 %copy-start.10 = (bf16[2,64,4,4,128]{4,3,2,1,0:T(4,128)(2,1)S(1)}, bf16[2,64,4,4,128]{4,3,2,1,0:T(4,128)(2,1)}, u32[]{:S(2)}) copy-start(bf16[2,64,4,4,128]{4,3,2,1,0:T(4,128)(2,1)} %reshape_squeeze.3) | copy-start | bytes 1572868
  35.5 5.9 %copy-start.28 = (s32[32]{0:T(128)S(1)}, s32[32]{0:T(128)}, u32[]{:S(2)}) copy-start(s32[32]{0:T(128)} %copy-done.27) | copy-start | bytes 388
  35.5 5.9 %copy-start.32 = (s32[32,1,2]{0,2,1:T(2,128)S(1)}, s32[32,1,2]{0,2,1:T(2,128)}, u32[]{:S(2)}) copy-start(s32[32,1,2]{0,2,1:T(2,128)} %copy-done.31) | copy-start | bytes 772
  46.1 37.7 %copy-start.33 = (s32[2,8]{1,0:T(2,128)S(1)}, s32[2,8]{1,0:T(2,128)}, u32[]{:S(2)}) copy-start(s32[2,8]{1,0:T(2,128)} %gather.33) | copy-start | bytes 196
  46.1 37.9 %copy-start.22 = (pred[2,64,128]{2,1,0:T(8,128)(4,1)S(1)}, pred[2,64,128]{2,1,0:T(8,128)(4,1)}, u32[]{:S(2)}) copy-start(pred[2,64,128]{2,1,0:T(8,128)(4,1)} %iota_compare_fusion) | copy-start | bytes 49156
  76.3 53.0 %all-to-all-start.2 = ((bf16[32,64,512]{2,1,0:T(8,128)(2,1)}), bf16[32,64,512]{2,1,0:T(8,128)(2,1)}, u32[]{:S(2)}, u32[]{:S(2)}) async-start(bf16[32,64,512]{2,1,0:T(8,128)(2,1)} %gather_fusion.3), calls=%async_computation.2 | async-start | bytes 4194304 | tf_op jit(solution)/shard_map/all_to_all | solution.py:129
  101.1 3.9 %copy-start.8 = (f32[16,64,256]{2,1,0:T(8,128)S(1)}, f32[16,64,256]{2,1,0:T(8,128)}, u32[]{:S(2)}) copy-start(f32[16,64,256]{2,1,0:T(8,128)} %reshape.409) | copy-start | bytes 3145732
  108.4 3.0 %copy-start.24 = (pred[32]{0:T(512)(128)(4,1)S(1)}, pred[32]{0:T(512)(128)(4,1)}, u32[]{:S(2)}) copy-start(pred[32]{0:T(512)(128)(4,1)} %get-tuple-element.50) | copy-start | bytes 100
  108.4 3.0 %copy-start.25 = (pred[32]{0:T(512)(128)(4,1)S(1)}, pred[32]{0:T(512)(128)(4,1)}, u32[]{:S(2)}) copy-start(pred[32]{0:T(512)(128)(4,1)} %get-tuple-element.51) | copy-start | bytes 100
  129.3 52.8 %all-to-all-start.3 = ((bf16[32,64,512]{2,1,0:T(8,128)(2,1)}), bf16[32,64,512]{2,1,0:T(8,128)(2,1)}, u32[]{:S(2)}, u32[]{:S(2)}) async-start(bf16[32,64,512]{2,1,0:T(8,128)(2,1)} %add_convert_fusion.1), calls=%async_computation.3 | async-start | bytes 4194304 | tf_op jit(solution)/shard_map/all_to_all | solution.py:177
  166.8 24.1 %copy-start.5 = (bf16[2,64,2,4,640]{4,1,3,2,0:T(8,128)(2,1)S(1)}, bf16[2,64,2,4,640]{4,1,3,2,0:T(8,128)(2,1)}, u32[]{:S(2)}) copy-start(bf16[2,64,2,4,640]{4,1,3,2,0:T(8,128)(2,1)} %copy-done.4) | copy-start | bytes 3932164
  166.8 24.1 %copy-start.18 = (bf16[2,2,128,128]{3,2,0,1:T(8,128)(2,1)S(1)}, bf16[2,2,128,128]{3,2,0,1:T(8,128)(2,1)}, u32[]{:S(2)}) copy-start(bf16[2,2,128,128]{3,2,0,1:T(8,128)(2,1)} %copy-done.17) | copy-start | bytes 393220
  182.2 53.5 %all-to-all-start.4 = ((bf16[32,64,512]{2,1,0:T(8,128)(2,1)}), bf16[32,64,512]{2,1,0:T(8,128)(2,1)S(1)}, u32[]{:S(2)}, u32[]{:S(2)}) async-start(bf16[32,64,512]{2,1,0:T(8,128)(2,1)} %add_convert_fusion), calls=%async_computation.4 | async-start | bytes 4194304 | tf_op jit(solution)/shard_map/all_to_all | solution.py:177
  192.5 8.1 %copy-start.7 = (bf16[2,64,2,4,640]{4,1,3,2,0:T(8,128)(2,1)S(1)}, bf16[2,64,2,4,640]{4,1,3,2,0:T(8,128)(2,1)}, u32[]{:S(2)}) copy-start(bf16[2,64,2,4,640]{4,1,3,2,0:T(8,128)(2,1)} %copy-done.6) | copy-start | bytes 3932164
  202.2 2.9 %copy-start.11 = (bf16[128,1024]{1,0:T(8,128)(2,1)S(1)}, bf16[128,1024]{1,0:T(8,128)(2,1)}, u32[]{:S(2)}) copy-start(bf16[128,1024]{1,0:T(8,128)(2,1)} %reshape.408) | copy-start | bytes 786436
  202.2 17.5 %copy-start.29 = (s32[32]{0:T(128)S(1)}, s32[32]{0:T(128)}, u32[]{:S(2)}) copy-start(s32[32]{0:T(128)} %get-tuple-element.44) | copy-start | bytes 388
  209.0 35.7 %collective-permute-start = (bf16[128,3072]{1,0:T(8,128)(2,1)}, bf16[128,3072]{1,0:T(8,128)(2,1)}, u32[]{:S(2)}, u32[]{:S(2)}) collective-permute-start(bf16[128,3072]{1,0:T(8,128)(2,1)} %constant_dynamic-update-slice_fusion.2), channel_id=1, source_target_pairs={{0,224},{32,0},{64,32},{96,64},{128,96},{160,128},{192,160},{224,1... | collective-permute-start | bytes 2359304 | tf_op jit(solution)/shard_map/ppermute | solution.py:189
  222.5 24.3 %collective-permute-start.1 = (f32[8,64,512]{2,0,1:T(8,128)S(1)}, f32[8,64,512]{2,0,1:T(8,128)}, u32[]{:S(2)}, u32[]{:S(2)}) collective-permute-start(f32[8,64,512]{2,0,1:T(8,128)S(1)} %fusion.8), channel_id=1, source_target_pairs={{0,256},{256,0},{1,257},{257,1},{2,258},{258,2},{3,259},{259,3},{4... | collective-permute-start | bytes 3145736 | tf_op jit(solution)/shard_map/ppermute | solution.py:183
  236.9 11.4 %collective-permute-start.2 = (f32[8,64,512]{2,0,1:T(8,128)S(1)}, f32[8,64,512]{2,0,1:T(8,128)S(1)}, u32[]{:S(2)}, u32[]{:S(2)}) collective-permute-start(f32[8,64,512]{2,0,1:T(8,128)S(1)} %fusion.6), channel_id=1, source_target_pairs={{0,256},{256,0},{1,257},{257,1},{2,258},{258,2},{3,259},{259,3},{4... | collective-permute-start | bytes 3145736 | tf_op jit(solution)/shard_map/ppermute | solution.py:183
  (18 other events, 23.0 us)

commit v4 on v3

--- a/solution.py
+++ b/solution.py
@@ -177,8 +177,13 @@
         received = lax.all_to_all(
             sent_grads[chunk], "mem", split_axis=0, concat_axis=0, tiled=True
         )
-        owned = jnp.einsum(
-            "rj,rtx->jtx", wanted_hot, received, preferred_element_type=jnp.float32
+        owned = jnp.sum(
+            jnp.where(
+                (wanted[None, :] == jnp.arange(held_blocks)[:, None])[:, :, None, None],
+                received.astype(jnp.float32)[None],
+                jnp.float32(0.0),
+            ),
+            axis=1,
         )
         partner = lax.ppermute(owned, "dp", [(0, 1), (1, 0)])
         owned_parts.append(owned + partner)

time: 252 us -> 260 us (1.032)
  other arithmetic: 26.8 us -> 38.2 us
  waiting for transfers between devices: 71.1 us -> 75.9 us
  matrix products: 14.5 us -> 10.4 us
  starting transfers between devices: 63.4 us -> 59.6 us
    reduce_sum x0 -> x1, other arithmetic: none -> 6.96 us  [per_device(): jnp.sum(jnp.where((wanted[None, :] == jnp.arange(held_blocks)[:, None])[:...]
    convert_element_type x0 -> x2, other arithmetic: none -> 4.66 us  [per_device(): received.astype(jnp.float32)[None]]
    all_to_all x2, waiting for transfers between devices: 22.6 us -> 27.1 us  [per_device(): lax.all_to_all(sent_grads[chunk], 'mem', split_axis=0, concat_axis=0, til...]
    dot_general x2 -> x0, matrix products: 4.06 us -> none  [per_device(): jnp.einsum('rj,rtx->jtx', wanted_hot, received, preferred_element_type=jn...]
    ppermute x2, starting transfers between devices: 13.6 us -> 9.75 us  [per_device(): partner = lax.ppermute(owned, 'dp', [(0, 1), (1, 0)])]
    unnamed x78 -> x79, local copies, waits for them, and re-layouts: 10.4 us -> 10.5 us
  transfers between devices with their start and end apart: 8 -> 8, of which waited for: 5 -> 6; matrix products, arithmetic and copies ran while one was open for 41% -> 42% of each run, Pallas kernels for 0% -> 0%
where the time goes in v4:
time: 260 us; the launch traced here: 259 us
  waiting for transfers between devices  75.9 us (29%)
  local copies, waits for them, and re-layouts  72.3 us (28%)
  starting transfers between devices  59.6 us (23%)
  other arithmetic  38.2 us (15%)
  matrix products  10.4 us (4%)
    all_to_all x2, waiting for transfers between devices, per_device(): lax.all_to_all(payload, 'mem', split_axis=0, concat_axis=0, tiled=True)  42.1 us
    all_to_all x2, waiting for transfers between devices, per_device(): lax.all_to_all(sent_grads[chunk], 'mem', split_axis=0, concat_axis=0, til...  27.1 us
    all_to_all x2, starting transfers between devices, per_device(): lax.all_to_all(sent_grads[chunk], 'mem', split_axis=0, concat_axis=0, til...  17 us
    convert_element_type x2, other arithmetic, per_device(): slot_grads = sum((jnp.where(present[block][:, None, None], by_block[block...  12.1 us
    gather x4, local copies, waits for them, and re-layouts, per_device(): by_block[block].at[key_slot[block]].get(mode='promise_in_bounds')  11.8 us
    all_to_all x2, starting transfers between devices, per_device(): lax.all_to_all(payload, 'mem', split_axis=0, concat_axis=0, tiled=True)  11.7 us
    ppermute x1, starting transfers between devices, per_device(): lax.ppermute(section_grads, 'section', [(i, (i - 1) % sections) for i in...  10.7 us
    unnamed x79, local copies, waits for them, and re-layouts  10.5 us
  transfers between devices with their start and end apart: 8, of which 6 were waited for; matrix products, arithmetic and copies ran while one was open for 42% of the time, Pallas kernels for 0%

profile of v4, /device:TPU:1, one launch (start us, length us, event | category | flops | bytes accessed | tf_op | source)
XLA Modules:
  0.0 258.6 jit_solution(130416835762228541)
XLA Ops:
  3.4 10.5 %all-to-all-start = ((s32[32,1,2]{2,1,0:T(1,128)}), s32[32,1,2]{2,1,0:T(1,128)S(1)}, u32[]{:S(2)}, u32[]{:S(2)}) async-start(s32[32,1,2]{2,1,0:T(1,128)} %copy.77), calls=%async_computation | async-start | bytes 32768 | tf_op jit(solution)/shard_map/all_to_all | solution.py:100
  15.9 6.5 %all-to-all-done = s32[32,1,2]{2,1,0:T(1,128)S(1)} async-done(((s32[32,1,2]{2,1,0:T(1,128)}), s32[32,1,2]{2,1,0:T(1,128)S(1)}, u32[]{:S(2)}, u32[]{:S(2)}) %all-to-all-start) | async-done | bytes 288 | tf_op jit(solution)/shard_map/all_to_all | solution.py:100
  25.1 4.1 %all-to-all-start.1 = ((bf16[32,64,512]{2,1,0:T(8,128)(2,1)}), bf16[32,64,512]{2,1,0:T(8,128)(2,1)S(1)}, u32[]{:S(2)}, u32[]{:S(2)}) async-start(bf16[32,64,512]{2,1,0:T(8,128)(2,1)} %gather_fusion), calls=%async_computation.1 | async-start | bytes 4194304 | tf_op jit(solution)/shard_map/all_to_all | solution.py:129
  32.6 2.2 reshape_squeeze.3
  46.1 30.2 %all-to-all-done.1 = bf16[32,64,512]{2,1,0:T(8,128)(2,1)S(1)} async-done(((bf16[32,64,512]{2,1,0:T(8,128)(2,1)}), bf16[32,64,512]{2,1,0:T(8,128)(2,1)S(1)}, u32[]{:S(2)}, u32[]{:S(2)}) %all-to-all-start.1) | async-done | bytes 2097184 | tf_op jit(solution)/shard_map/all_to_all | solution.py:129
  76.3 7.6 %all-to-all-start.2 = ((bf16[32,64,512]{2,1,0:T(8,128)(2,1)}), bf16[32,64,512]{2,1,0:T(8,128)(2,1)}, u32[]{:S(2)}, u32[]{:S(2)}) async-start(bf16[32,64,512]{2,1,0:T(8,128)(2,1)} %gather_fusion.3), calls=%async_computation.2 | async-start | bytes 4194304 | tf_op jit(solution)/shard_map/all_to_all | solution.py:129
  96.0 3.0 %reshape.431 = f32[16,64,256]{2,1,0:T(8,128)} reshape(f32[2,512,2,128]{3,2,1,0:T(2,128)} %copy.86) | data formatting | bytes 2097152 | tf_op jit(solution)/shard_map/reshape | solution.py:161
  105.4 3.0 %gather_fusion.4 = f32[32,64,512]{2,1,0:T(8,128)} fusion(f32[8,64,512]{2,1,0:T(8,128)S(1)} %get-tuple-element.12, s32[1024]{0:T(1024)} %get-tuple-element.51), kind=kCustom, calls=%fused_computation.4 | custom fusion | bytes 8388736 | tf_op jit(solution)/shard_map/gather | solution.py:170
  108.4 3.0 %gather_fusion.5 = f32[32,64,512]{2,1,0:T(8,128)} fusion(f32[8,64,512]{2,1,0:T(8,128)S(1)} %get-tuple-element.13, s32[1024]{0:T(1024)} %get-tuple-element.50), kind=kCustom, calls=%fused_computation.5 | custom fusion | bytes 8388736 | tf_op jit(solution)/shard_map/gather | solution.py:170
  111.4 6.1 %add_convert_fusion.1 = bf16[32,64,512]{2,1,0:T(8,128)(2,1)} fusion(f32[32,64,512]{2,1,0:T(8,128)} %gather_fusion.5, f32[32,64,512]{2,1,0:T(8,128)} %gather_fusion.4, pred[32]{0:T(512)(128)(4,1)S(1)} %copy-done.26, pred[32]{0:T(512)(128)(4,1)S(1)} %copy-done.25), kind=kLoop, calls=%fused_computation.12 | loop fusion | flops 4194304 | bytes 10485824 | tf_op jit(solution)/shard_map/convert_element_type | solution.py:174
  117.5 11.9 %all-to-all-done.2 = bf16[32,64,512]{2,1,0:T(8,128)(2,1)} async-done(((bf16[32,64,512]{2,1,0:T(8,128)(2,1)}), bf16[32,64,512]{2,1,0:T(8,128)(2,1)}, u32[]{:S(2)}, u32[]{:S(2)}) %all-to-all-start.2) | async-done | bytes 2097184 | tf_op jit(solution)/shard_map/all_to_all | solution.py:129
  129.3 8.2 %all-to-all-start.3 = ((bf16[32,64,512]{2,1,0:T(8,128)(2,1)}), bf16[32,64,512]{2,1,0:T(8,128)(2,1)}, u32[]{:S(2)}, u32[]{:S(2)}) async-start(bf16[32,64,512]{2,1,0:T(8,128)(2,1)} %add_convert_fusion.1), calls=%async_computation.3 | async-start | bytes 4194304 | tf_op jit(solution)/shard_map/all_to_all | solution.py:177
  137.5 2.2 gather_fusion.6
  147.6 3.1 %reshape.439 = f32[16,64,256]{2,1,0:T(8,128)} reshape(f32[2,512,2,128]{3,2,1,0:T(2,128)} %copy.103) | data formatting | bytes 2097152 | tf_op jit(solution)/shard_map/reshape | solution.py:161
  155.0 2.9 %gather_fusion.7 = f32[32,64,512]{2,1,0:T(8,128)} fusion(f32[8,64,512]{2,1,0:T(8,128)S(1)} %get-tuple-element.10, s32[1024]{0:T(1024)} %get-tuple-element.51), kind=kCustom, calls=%fused_computation.7 | custom fusion | bytes 8388736 | tf_op jit(solution)/shard_map/gather | solution.py:170
  157.8 3.0 %gather_fusion.8 = f32[32,64,512]{2,1,0:T(8,128)} fusion(f32[8,64,512]{2,1,0:T(8,128)S(1)} %get-tuple-element.11, s32[1024]{0:T(1024)} %get-tuple-element.50), kind=kCustom, calls=%fused_computation.8 | custom fusion | bytes 8388736 | tf_op jit(solution)/shard_map/gather | solution.py:170
  160.8 6.0 %add_convert_fusion = bf16[32,64,512]{2,1,0:T(8,128)(2,1)} fusion(f32[32,64,512]{2,1,0:T(8,128)} %gather_fusion.8, f32[32,64,512]{2,1,0:T(8,128)} %gather_fusion.7, pred[32]{0:T(512)(128)(4,1)S(1)} %copy-done.26, pred[32]{0:T(512)(128)(4,1)S(1)} %copy-done.25), kind=kLoop, calls=%fused_computation.11 | loop fusion | flops 4194304 | bytes 10485824 | tf_op jit(solution)/shard_map/convert_element_type | solution.py:174
  166.8 15.3 %all-to-all-done.3 = bf16[32,64,512]{2,1,0:T(8,128)(2,1)} async-done(((bf16[32,64,512]{2,1,0:T(8,128)(2,1)}), bf16[32,64,512]{2,1,0:T(8,128)(2,1)}, u32[]{:S(2)}, u32[]{:S(2)}) %all-to-all-start.3) | async-done | bytes 2097184 | tf_op jit(solution)/shard_map/all_to_all | solution.py:177
  182.1 8.8 %all-to-all-start.4 = ((bf16[32,64,512]{2,1,0:T(8,128)(2,1)}), bf16[32,64,512]{2,1,0:T(8,128)(2,1)S(1)}, u32[]{:S(2)}, u32[]{:S(2)}) async-start(bf16[32,64,512]{2,1,0:T(8,128)(2,1)} %add_convert_fusion), calls=%async_computation.4 | async-start | bytes 4194304 | tf_op jit(solution)/shard_map/all_to_all | solution.py:177
  209.0 10.7 %collective-permute-start = (bf16[128,3072]{1,0:T(8,128)(2,1)}, bf16[128,3072]{1,0:T(8,128)(2,1)}, u32[]{:S(2)}, u32[]{:S(2)}) collective-permute-start(bf16[128,3072]{1,0:T(8,128)(2,1)} %constant_dynamic-update-slice_fusion.2), channel_id=1, source_target_pairs={{0,224},{32,0},{64,32},{96,64},{128,96},{160,128},{192,160},{224,1... | collective-permute-start | bytes 2359304 | tf_op jit(solution)/shard_map/ppermute | solution.py:194
  219.7 4.1 %convert_element_type.74 = f32[32,64,512]{2,1,0:T(8,128)} convert(bf16[32,64,512]{2,1,0:T(8,128)(2,1)} %all-to-all-done.3) | non-fusion elementwise | flops 1048576 | bytes 6291456 | tf_op jit(solution)/shard_map/convert_element_type | solution.py:183
  223.8 11.8 %all-to-all-done.4 = bf16[32,64,512]{2,1,0:T(8,128)(2,1)S(1)} async-done(((bf16[32,64,512]{2,1,0:T(8,128)(2,1)}), bf16[32,64,512]{2,1,0:T(8,128)(2,1)S(1)}, u32[]{:S(2)}, u32[]{:S(2)}) %all-to-all-start.4) | async-done | bytes 2097184 | tf_op jit(solution)/shard_map/all_to_all | solution.py:177
  237.8 7.0 %select_reduce_fusion.1 = (f32[8,64,512]{2,1,0:T(8,128)S(1)}, f32[8,64,512]{2,1,0:T(8,128)S(1)}) fusion(f32[32,64,512]{2,1,0:T(8,128)S(1)} %copy-done, pred[8,32]{1,0:T(8,128)(4,1)S(1)} %iota_compare_fusion.2, f32[32,64,512]{2,1,0:T(8,128)S(1)} %convert_element_type.76), kind=kLoop, calls=%fused_computation.10 | loop fusion | flops 33030144 | bytes 10486016 | tf_op jit(solution)/shard_map/reduce_sum | solution.py:180
  244.8 7.8 %collective-permute-start.1 = (f32[8,64,512]{2,1,0:T(8,128)S(1)}, f32[8,64,512]{2,1,0:T(8,128)S(1)}, u32[]{:S(2)}, u32[]{:S(2)}) collective-permute-start(f32[8,64,512]{2,1,0:T(8,128)S(1)} %get-tuple-element.6), channel_id=1, source_target_pairs={{0,256},{256,0},{1,257},{257,1},{2,258},{258,2},{3,259},{259,3},{4... | collective-permute-start | bytes 3145736 | tf_op jit(solution)/shard_map/ppermute | solution.py:188
  (192 shorter events, 77.6 us)
Async XLA Ops:
  2.6 13.2 %copy-start.28 = (s32[32]{0:T(128)}, s32[32]{0:T(128)S(1)}, u32[]{:S(2)}) copy-start(s32[32]{0:T(128)S(1)} %get-tuple-element.9) | copy-start | bytes 388
  3.4 19.0 %all-to-all-start = ((s32[32,1,2]{2,1,0:T(1,128)}), s32[32,1,2]{2,1,0:T(1,128)S(1)}, u32[]{:S(2)}, u32[]{:S(2)}) async-start(s32[32,1,2]{2,1,0:T(1,128)} %copy.77), calls=%async_computation | async-start | bytes 32768 | tf_op jit(solution)/shard_map/all_to_all | solution.py:100
  25.1 4.2 %copy-start.30 = (s32[1,1,2,8]{3,2,1,0:T(2,128)S(1)}, s32[1,1,2,8]{3,2,1,0:T(2,128)}, u32[]{:S(2)}) copy-start(s32[1,1,2,8]{3,2,1,0:T(2,128)} %param.9) | copy-start | bytes 196
  25.1 51.2 %all-to-all-start.1 = ((bf16[32,64,512]{2,1,0:T(8,128)(2,1)}), bf16[32,64,512]{2,1,0:T(8,128)(2,1)S(1)}, u32[]{:S(2)}, u32[]{:S(2)}) async-start(bf16[32,64,512]{2,1,0:T(8,128)(2,1)} %gather_fusion), calls=%async_computation.1 | async-start | bytes 4194304 | tf_op jit(solution)/shard_map/all_to_all | solution.py:129
  29.4 5.4 %copy-start.27 = (s32[2,32]{1,0:T(2,128)S(1)}, s32[2,32]{1,0:T(2,128)}, u32[]{:S(2)}) copy-start(s32[2,32]{1,0:T(2,128)} %get-tuple-element.8) | copy-start | bytes 772
  34.8 6.4 %copy-start.11 = (bf16[2,64,4,4,128]{4,3,2,1,0:T(4,128)(2,1)S(1)}, bf16[2,64,4,4,128]{4,3,2,1,0:T(4,128)(2,1)}, u32[]{:S(2)}) copy-start(bf16[2,64,4,4,128]{4,3,2,1,0:T(4,128)(2,1)} %reshape_squeeze.3) | copy-start | bytes 1572868
  35.5 5.8 %copy-start.29 = (s32[32]{0:T(128)S(1)}, s32[32]{0:T(128)}, u32[]{:S(2)}) copy-start(s32[32]{0:T(128)} %copy-done.28) | copy-start | bytes 388
  35.5 5.8 %copy-start.32 = (s32[32,1,2]{0,2,1:T(2,128)S(1)}, s32[32,1,2]{0,2,1:T(2,128)}, u32[]{:S(2)}) copy-start(s32[32,1,2]{0,2,1:T(2,128)} %copy-done.31) | copy-start | bytes 772
  46.1 37.8 %copy-start.33 = (s32[2,8]{1,0:T(2,128)S(1)}, s32[2,8]{1,0:T(2,128)}, u32[]{:S(2)}) copy-start(s32[2,8]{1,0:T(2,128)} %gather.33) | copy-start | bytes 196
  46.1 38.0 %copy-start.23 = (pred[2,64,128]{2,1,0:T(8,128)(4,1)S(1)}, pred[2,64,128]{2,1,0:T(8,128)(4,1)}, u32[]{:S(2)}) copy-start(pred[2,64,128]{2,1,0:T(8,128)(4,1)} %iota_compare_fusion) | copy-start | bytes 49156
  76.3 53.0 %all-to-all-start.2 = ((bf16[32,64,512]{2,1,0:T(8,128)(2,1)}), bf16[32,64,512]{2,1,0:T(8,128)(2,1)}, u32[]{:S(2)}, u32[]{:S(2)}) async-start(bf16[32,64,512]{2,1,0:T(8,128)(2,1)} %gather_fusion.3), calls=%async_computation.2 | async-start | bytes 4194304 | tf_op jit(solution)/shard_map/all_to_all | solution.py:129
  101.1 3.9 %copy-start.9 = (f32[16,64,256]{2,1,0:T(8,128)S(1)}, f32[16,64,256]{2,1,0:T(8,128)}, u32[]{:S(2)}) copy-start(f32[16,64,256]{2,1,0:T(8,128)} %reshape.431) | copy-start | bytes 3145732
  108.4 3.0 %copy-start.25 = (pred[32]{0:T(512)(128)(4,1)S(1)}, pred[32]{0:T(512)(128)(4,1)}, u32[]{:S(2)}) copy-start(pred[32]{0:T(512)(128)(4,1)} %get-tuple-element.42) | copy-start | bytes 100
  108.4 3.0 %copy-start.26 = (pred[32]{0:T(512)(128)(4,1)S(1)}, pred[32]{0:T(512)(128)(4,1)}, u32[]{:S(2)}) copy-start(pred[32]{0:T(512)(128)(4,1)} %get-tuple-element.43) | copy-start | bytes 100
  129.3 52.8 %all-to-all-start.3 = ((bf16[32,64,512]{2,1,0:T(8,128)(2,1)}), bf16[32,64,512]{2,1,0:T(8,128)(2,1)}, u32[]{:S(2)}, u32[]{:S(2)}) async-start(bf16[32,64,512]{2,1,0:T(8,128)(2,1)} %add_convert_fusion.1), calls=%async_computation.3 | async-start | bytes 4194304 | tf_op jit(solution)/shard_map/all_to_all | solution.py:177
  166.8 24.1 %copy-start.34 = (s32[32]{0:T(128)S(1)}, s32[32]{0:T(128)}, u32[]{:S(2)}) copy-start(s32[32]{0:T(128)} %get-tuple-element.36) | copy-start | bytes 388
  166.8 24.1 %copy-start.6 = (bf16[2,64,2,4,640]{4,1,3,2,0:T(8,128)(2,1)S(1)}, bf16[2,64,2,4,640]{4,1,3,2,0:T(8,128)(2,1)}, u32[]{:S(2)}) copy-start(bf16[2,64,2,4,640]{4,1,3,2,0:T(8,128)(2,1)} %copy-done.5) | copy-start | bytes 3932164
  166.8 24.1 %copy-start.19 = (bf16[2,2,128,128]{3,2,0,1:T(8,128)(2,1)S(1)}, bf16[2,2,128,128]{3,2,0,1:T(8,128)(2,1)}, u32[]{:S(2)}) copy-start(bf16[2,2,128,128]{3,2,0,1:T(8,128)(2,1)} %copy-done.18) | copy-start | bytes 393220
  182.1 53.5 %all-to-all-start.4 = ((bf16[32,64,512]{2,1,0:T(8,128)(2,1)}), bf16[32,64,512]{2,1,0:T(8,128)(2,1)S(1)}, u32[]{:S(2)}, u32[]{:S(2)}) async-start(bf16[32,64,512]{2,1,0:T(8,128)(2,1)} %add_convert_fusion), calls=%async_computation.4 | async-start | bytes 4194304 | tf_op jit(solution)/shard_map/all_to_all | solution.py:177
  192.5 8.1 %copy-start.8 = (bf16[2,64,2,4,640]{4,1,3,2,0:T(8,128)(2,1)S(1)}, bf16[2,64,2,4,640]{4,1,3,2,0:T(8,128)(2,1)}, u32[]{:S(2)}) copy-start(bf16[2,64,2,4,640]{4,1,3,2,0:T(8,128)(2,1)} %copy-done.7) | copy-start | bytes 3932164
  202.2 2.8 %copy-start.12 = (bf16[128,1024]{1,0:T(8,128)(2,1)S(1)}, bf16[128,1024]{1,0:T(8,128)(2,1)}, u32[]{:S(2)}) copy-start(bf16[128,1024]{1,0:T(8,128)(2,1)} %reshape.430) | copy-start | bytes 786436
  209.0 45.5 %collective-permute-start = (bf16[128,3072]{1,0:T(8,128)(2,1)}, bf16[128,3072]{1,0:T(8,128)(2,1)}, u32[]{:S(2)}, u32[]{:S(2)}) collective-permute-start(bf16[128,3072]{1,0:T(8,128)(2,1)} %constant_dynamic-update-slice_fusion.2), channel_id=1, source_target_pairs={{0,224},{32,0},{64,32},{96,64},{128,96},{160,128},{192,160},{224,1... | collective-permute-start | bytes 2359304 | tf_op jit(solution)/shard_map/ppermute | solution.py:194
  244.8 11.9 %collective-permute-start.1 = (f32[8,64,512]{2,1,0:T(8,128)S(1)}, f32[8,64,512]{2,1,0:T(8,128)S(1)}, u32[]{:S(2)}, u32[]{:S(2)}) collective-permute-start(f32[8,64,512]{2,1,0:T(8,128)S(1)} %get-tuple-element.6), channel_id=1, source_target_pairs={{0,256},{256,0},{1,257},{257,1},{2,258},{258,2},{3,259},{259,3},{4... | collective-permute-start | bytes 3145736 | tf_op jit(solution)/shard_map/ppermute | solution.py:188
  252.6 4.6 %collective-permute-start.2 = (f32[8,64,512]{2,1,0:T(8,128)S(1)}, f32[8,64,512]{2,1,0:T(8,128)S(1)}, u32[]{:S(2)}, u32[]{:S(2)}) collective-permute-start(f32[8,64,512]{2,1,0:T(8,128)S(1)} %get-tuple-element.7), channel_id=1, source_target_pairs={{0,256},{256,0},{1,257},{257,1},{2,258},{258,2},{3,259},{259,3},{4... | collective-permute-start | bytes 3145736 | tf_op jit(solution)/shard_map/ppermute | solution.py:188
  (19 other events, 25.1 us)

commit v5 on v3

--- a/solution.py
+++ b/solution.py
@@ -96,7 +96,8 @@
     shard_ids = jnp.arange(shards, dtype=jnp.int32)
     hits = owner_shard[:, :, None] == shard_ids[None, None, :]
     request = jnp.max(jnp.where(hits, slot_index[:, :, None], -1), axis=(0, 1))
-    asks = jnp.stack([request, jnp.broadcast_to(shard_fill[0, 0], (shards,))], axis=1)
+    lanes = jnp.arange(128)[None, :]
+    asks = jnp.where(lanes == 0, request[:, None], shard_fill[0, 0])
     answers = lax.all_to_all(asks, "mem", split_axis=0, concat_axis=0, tiled=True)
     wanted = answers[:, 0]
     fills = answers[:, 1]

time: 252 us -> 252 us (level)
    unnamed x78 -> x76, local copies, waits for them, and re-layouts: 10.4 us -> 11 us
where the time goes in v5:
time: 252 us; the launch traced here: 251 us
  local copies, waits for them, and re-layouts  72.3 us (29%)
  waiting for transfers between devices  70.3 us (28%)
  starting transfers between devices  63.5 us (25%)
  other arithmetic  28.1 us (11%)
  matrix products  14.4 us (6%)
    all_to_all x2, waiting for transfers between devices, per_device(): lax.all_to_all(payload, 'mem', split_axis=0, concat_axis=0, tiled=True)  41.2 us
    all_to_all x2, waiting for transfers between devices, per_device(): lax.all_to_all(sent_grads[chunk], 'mem', split_axis=0, concat_axis=0, til...  22.6 us
    all_to_all x2, starting transfers between devices, per_device(): lax.all_to_all(sent_grads[chunk], 'mem', split_axis=0, concat_axis=0, til...  17 us
    ppermute x2, starting transfers between devices, per_device(): partner = lax.ppermute(owned, 'dp', [(0, 1), (1, 0)])  13.6 us
    convert_element_type x2, other arithmetic, per_device(): slot_grads = sum((jnp.where(present[block][:, None, None], by_block[block...  12.1 us
    gather x4, local copies, waits for them, and re-layouts, per_device(): by_block[block].at[key_slot[block]].get(mode='promise_in_bounds')  11.8 us
    all_to_all x2, starting transfers between devices, per_device(): lax.all_to_all(payload, 'mem', split_axis=0, concat_axis=0, tiled=True)  11.7 us
    unnamed x76, local copies, waits for them, and re-layouts  11 us
  transfers between devices with their start and end apart: 8, of which 5 were waited for; matrix products, arithmetic and copies ran while one was open for 41% of the time, Pallas kernels for 0%

profile of v5, /device:TPU:1, one launch (start us, length us, event | category | flops | bytes accessed | tf_op | source)
XLA Modules:
  0.0 250.8 jit_solution(15645886748596270339)
XLA Ops:
  3.9 10.5 %all-to-all-start = ((s32[32,1,128]{2,1,0:T(1,128)}), s32[32,1,128]{2,1,0:T(1,128)S(1)}, u32[]{:S(2)}, u32[]{:S(2)}) async-start(s32[32,1,128]{2,1,0:T(1,128)} %broadcast_select_fusion), calls=%async_computation | async-start | bytes 32768 | tf_op jit(solution)/shard_map/all_to_all | solution.py:101
  16.4 6.5 %all-to-all-done = s32[32,1,128]{2,1,0:T(1,128)S(1)} async-done(((s32[32,1,128]{2,1,0:T(1,128)}), s32[32,1,128]{2,1,0:T(1,128)S(1)}, u32[]{:S(2)}, u32[]{:S(2)}) %all-to-all-start) | async-done | bytes 16416 | tf_op jit(solution)/shard_map/all_to_all | solution.py:101
  25.6 4.2 %all-to-all-start.1 = ((bf16[32,64,512]{2,1,0:T(8,128)(2,1)}), bf16[32,64,512]{2,1,0:T(8,128)(2,1)S(1)}, u32[]{:S(2)}, u32[]{:S(2)}) async-start(bf16[32,64,512]{2,1,0:T(8,128)(2,1)} %gather_fusion), calls=%async_computation.1 | async-start | bytes 4194304 | tf_op jit(solution)/shard_map/all_to_all | solution.py:130
  33.1 2.2 reshape_squeeze.3
  47.4 29.4 %all-to-all-done.1 = bf16[32,64,512]{2,1,0:T(8,128)(2,1)S(1)} async-done(((bf16[32,64,512]{2,1,0:T(8,128)(2,1)}), bf16[32,64,512]{2,1,0:T(8,128)(2,1)S(1)}, u32[]{:S(2)}, u32[]{:S(2)}) %all-to-all-start.1) | async-done | bytes 2097184 | tf_op jit(solution)/shard_map/all_to_all | solution.py:130
  76.8 7.6 %all-to-all-start.2 = ((bf16[32,64,512]{2,1,0:T(8,128)(2,1)}), bf16[32,64,512]{2,1,0:T(8,128)(2,1)}, u32[]{:S(2)}, u32[]{:S(2)}) async-start(bf16[32,64,512]{2,1,0:T(8,128)(2,1)} %gather_fusion.3), calls=%async_computation.2 | async-start | bytes 4194304 | tf_op jit(solution)/shard_map/all_to_all | solution.py:130
  96.5 3.0 %reshape.453 = f32[16,64,256]{2,1,0:T(8,128)} reshape(f32[2,512,2,128]{3,2,1,0:T(2,128)} %copy.95) | data formatting | bytes 2097152 | tf_op jit(solution)/shard_map/reshape | solution.py:162
  106.0 3.0 %gather_fusion.4 = f32[32,64,512]{2,1,0:T(8,128)} fusion(f32[8,64,512]{2,1,0:T(8,128)S(1)} %get-tuple-element.20, s32[1024]{0:T(1024)} %get-tuple-element.59), kind=kCustom, calls=%fused_computation.4 | custom fusion | bytes 8388736 | tf_op jit(solution)/shard_map/gather | solution.py:171
  108.9 3.0 %gather_fusion.5 = f32[32,64,512]{2,1,0:T(8,128)} fusion(f32[8,64,512]{2,1,0:T(8,128)S(1)} %get-tuple-element.21, s32[1024]{0:T(1024)} %get-tuple-element.58), kind=kCustom, calls=%fused_computation.5 | custom fusion | bytes 8388736 | tf_op jit(solution)/shard_map/gather | solution.py:171
  112.0 6.1 %add_convert_fusion.1 = bf16[32,64,512]{2,1,0:T(8,128)(2,1)} fusion(f32[32,64,512]{2,1,0:T(8,128)} %gather_fusion.5, f32[32,64,512]{2,1,0:T(8,128)} %gather_fusion.4, pred[32]{0:T(512)(128)(4,1)S(1)} %copy-done.26, pred[32]{0:T(512)(128)(4,1)S(1)} %copy-done.25), kind=kLoop, calls=%fused_computation.10 | loop fusion | flops 4194304 | bytes 10485824 | tf_op jit(solution)/shard_map/convert_element_type | solution.py:175
  118.0 11.8 %all-to-all-done.2 = bf16[32,64,512]{2,1,0:T(8,128)(2,1)} async-done(((bf16[32,64,512]{2,1,0:T(8,128)(2,1)}), bf16[32,64,512]{2,1,0:T(8,128)(2,1)}, u32[]{:S(2)}, u32[]{:S(2)}) %all-to-all-start.2) | async-done | bytes 2097184 | tf_op jit(solution)/shard_map/all_to_all | solution.py:130
  129.8 8.2 %all-to-all-start.3 = ((bf16[32,64,512]{2,1,0:T(8,128)(2,1)}), bf16[32,64,512]{2,1,0:T(8,128)(2,1)}, u32[]{:S(2)}, u32[]{:S(2)}) async-start(bf16[32,64,512]{2,1,0:T(8,128)(2,1)} %add_convert_fusion.1), calls=%async_computation.3 | async-start | bytes 4194304 | tf_op jit(solution)/shard_map/all_to_all | solution.py:178
  138.0 2.2 gather_fusion.6
  148.1 3.1 %reshape.461 = f32[16,64,256]{2,1,0:T(8,128)} reshape(f32[2,512,2,128]{3,2,1,0:T(2,128)} %copy.113) | data formatting | bytes 2097152 | tf_op jit(solution)/shard_map/reshape | solution.py:162
  155.5 2.9 %gather_fusion.7 = f32[32,64,512]{2,1,0:T(8,128)} fusion(f32[8,64,512]{2,1,0:T(8,128)S(1)} %get-tuple-element.18, s32[1024]{0:T(1024)} %get-tuple-element.59), kind=kCustom, calls=%fused_computation.7 | custom fusion | bytes 8388736 | tf_op jit(solution)/shard_map/gather | solution.py:171
  158.3 3.0 %gather_fusion.8 = f32[32,64,512]{2,1,0:T(8,128)} fusion(f32[8,64,512]{2,1,0:T(8,128)S(1)} %get-tuple-element.19, s32[1024]{0:T(1024)} %get-tuple-element.58), kind=kCustom, calls=%fused_computation.8 | custom fusion | bytes 8388736 | tf_op jit(solution)/shard_map/gather | solution.py:171
  161.3 6.0 %add_convert_fusion = bf16[32,64,512]{2,1,0:T(8,128)(2,1)} fusion(f32[32,64,512]{2,1,0:T(8,128)} %gather_fusion.8, f32[32,64,512]{2,1,0:T(8,128)} %gather_fusion.7, pred[32]{0:T(512)(128)(4,1)S(1)} %copy-done.26, pred[32]{0:T(512)(128)(4,1)S(1)} %copy-done.25), kind=kLoop, calls=%fused_computation.9 | loop fusion | flops 4194304 | bytes 10485824 | tf_op jit(solution)/shard_map/convert_element_type | solution.py:175
  167.3 15.3 %all-to-all-done.3 = bf16[32,64,512]{2,1,0:T(8,128)(2,1)} async-done(((bf16[32,64,512]{2,1,0:T(8,128)(2,1)}), bf16[32,64,512]{2,1,0:T(8,128)(2,1)}, u32[]{:S(2)}, u32[]{:S(2)}) %all-to-all-start.3) | async-done | bytes 2097184 | tf_op jit(solution)/shard_map/all_to_all | solution.py:178
  182.7 8.8 %all-to-all-start.4 = ((bf16[32,64,512]{2,1,0:T(8,128)(2,1)}), bf16[32,64,512]{2,1,0:T(8,128)(2,1)S(1)}, u32[]{:S(2)}, u32[]{:S(2)}) async-start(bf16[32,64,512]{2,1,0:T(8,128)(2,1)} %add_convert_fusion), calls=%async_computation.4 | async-start | bytes 4194304 | tf_op jit(solution)/shard_map/all_to_all | solution.py:178
  209.5 10.7 %collective-permute-start = (bf16[128,3072]{1,0:T(8,128)(2,1)}, bf16[128,3072]{1,0:T(8,128)(2,1)}, u32[]{:S(2)}, u32[]{:S(2)}) collective-permute-start(bf16[128,3072]{1,0:T(8,128)(2,1)} %constant_dynamic-update-slice_fusion.2), channel_id=1, source_target_pairs={{0,224},{32,0},{64,32},{96,64},{128,96},{160,128},{192,160},{224,1... | collective-permute-start | bytes 2359304 | tf_op jit(solution)/shard_map/ppermute | solution.py:190
  220.2 2.8 %fusion.8 = f32[8,64,512]{2,0,1:T(8,128)S(1)} fusion(bf16[32,64,512]{2,1,0:T(8,128)(2,1)} %all-to-all-done.3, s32[32]{0:T(128)S(1)} %copy-done.30), kind=kOutput, calls=%fused_computation.27 | convolution fusion | flops 16777472 | bytes 3145856 | tf_op jit(solution)/shard_map/rj,rtx->jtx/dot_general | solution.py:181
  223.0 5.8 %collective-permute-start.1 = (f32[8,64,512]{2,0,1:T(8,128)S(1)}, f32[8,64,512]{2,0,1:T(8,128)}, u32[]{:S(2)}, u32[]{:S(2)}) collective-permute-start(f32[8,64,512]{2,0,1:T(8,128)S(1)} %fusion.8), channel_id=1, source_target_pairs={{0,256},{256,0},{1,257},{257,1},{2,258},{258,2},{3,259},{259,3},{4... | collective-permute-start | bytes 3145736 | tf_op jit(solution)/shard_map/ppermute | solution.py:184
  228.9 7.3 %all-to-all-done.4 = bf16[32,64,512]{2,1,0:T(8,128)(2,1)S(1)} async-done(((bf16[32,64,512]{2,1,0:T(8,128)(2,1)}), bf16[32,64,512]{2,1,0:T(8,128)(2,1)S(1)}, u32[]{:S(2)}, u32[]{:S(2)}) %all-to-all-start.4) | async-done | bytes 2097184 | tf_op jit(solution)/shard_map/all_to_all | solution.py:178
  237.4 7.8 %collective-permute-start.2 = (f32[8,64,512]{2,0,1:T(8,128)S(1)}, f32[8,64,512]{2,0,1:T(8,128)S(1)}, u32[]{:S(2)}, u32[]{:S(2)}) collective-permute-start(f32[8,64,512]{2,0,1:T(8,128)S(1)} %fusion.6), channel_id=1, source_target_pairs={{0,256},{256,0},{1,257},{257,1},{2,258},{258,2},{3,259},{259,3},{4... | collective-permute-start | bytes 3145736 | tf_op jit(solution)/shard_map/ppermute | solution.py:184
  (187 shorter events, 77.6 us)
Async XLA Ops:
  3.9 19.0 %all-to-all-start = ((s32[32,1,128]{2,1,0:T(1,128)}), s32[32,1,128]{2,1,0:T(1,128)S(1)}, u32[]{:S(2)}, u32[]{:S(2)}) async-start(s32[32,1,128]{2,1,0:T(1,128)} %broadcast_select_fusion), calls=%async_computation | async-start | bytes 32768 | tf_op jit(solution)/shard_map/all_to_all | solution.py:101
  23.0 2.6 %copy-start.22 = (s32[32,1,128]{0,2,1:T(8,128)}, s32[32,1,128]{0,2,1:T(8,128)S(1)}, u32[]{:S(2)}) copy-start(s32[32,1,128]{0,2,1:T(8,128)S(1)} %copy.87) | copy-start | bytes 49156
  23.6 2.0 copy-start.24
  25.6 4.2 %copy-start.31 = (s32[1,1,2,8]{3,2,1,0:T(2,128)S(1)}, s32[1,1,2,8]{3,2,1,0:T(2,128)}, u32[]{:S(2)}) copy-start(s32[1,1,2,8]{3,2,1,0:T(2,128)} %param.9) | copy-start | bytes 196
  25.6 51.2 %all-to-all-start.1 = ((bf16[32,64,512]{2,1,0:T(8,128)(2,1)}), bf16[32,64,512]{2,1,0:T(8,128)(2,1)S(1)}, u32[]{:S(2)}, u32[]{:S(2)}) async-start(bf16[32,64,512]{2,1,0:T(8,128)(2,1)} %gather_fusion), calls=%async_computation.1 | async-start | bytes 4194304 | tf_op jit(solution)/shard_map/all_to_all | solution.py:130
  30.0 5.4 %copy-start.27 = (s32[2,32]{1,0:T(2,128)S(1)}, s32[2,32]{1,0:T(2,128)}, u32[]{:S(2)}) copy-start(s32[2,32]{1,0:T(2,128)} %get-tuple-element.16) | copy-start | bytes 772
  35.3 6.5 %copy-start.10 = (bf16[2,64,4,4,128]{4,3,2,1,0:T(4,128)(2,1)S(1)}, bf16[2,64,4,4,128]{4,3,2,1,0:T(4,128)(2,1)}, u32[]{:S(2)}) copy-start(bf16[2,64,4,4,128]{4,3,2,1,0:T(4,128)(2,1)} %reshape_squeeze.3) | copy-start | bytes 1572868
  36.1 5.9 %copy-start.29 = (s32[32]{0:T(128)S(1)}, s32[32]{0:T(128)}, u32[]{:S(2)}) copy-start(s32[32]{0:T(128)} %copy-done.28) | copy-start | bytes 388
  47.4 37.0 %copy-start.32 = (s32[2,8]{1,0:T(2,128)S(1)}, s32[2,8]{1,0:T(2,128)}, u32[]{:S(2)}) copy-start(s32[2,8]{1,0:T(2,128)} %gather.33) | copy-start | bytes 196
  47.4 37.2 %copy-start.23 = (pred[2,64,128]{2,1,0:T(8,128)(4,1)S(1)}, pred[2,64,128]{2,1,0:T(8,128)(4,1)}, u32[]{:S(2)}) copy-start(pred[2,64,128]{2,1,0:T(8,128)(4,1)} %iota_compare_fusion) | copy-start | bytes 49156
  76.8 53.0 %all-to-all-start.2 = ((bf16[32,64,512]{2,1,0:T(8,128)(2,1)}), bf16[32,64,512]{2,1,0:T(8,128)(2,1)}, u32[]{:S(2)}, u32[]{:S(2)}) async-start(bf16[32,64,512]{2,1,0:T(8,128)(2,1)} %gather_fusion.3), calls=%async_computation.2 | async-start | bytes 4194304 | tf_op jit(solution)/shard_map/all_to_all | solution.py:130
  101.6 3.9 %copy-start.8 = (f32[16,64,256]{2,1,0:T(8,128)S(1)}, f32[16,64,256]{2,1,0:T(8,128)}, u32[]{:S(2)}) copy-start(f32[16,64,256]{2,1,0:T(8,128)} %reshape.453) | copy-start | bytes 3145732
  108.9 3.0 %copy-start.25 = (pred[32]{0:T(512)(128)(4,1)S(1)}, pred[32]{0:T(512)(128)(4,1)}, u32[]{:S(2)}) copy-start(pred[32]{0:T(512)(128)(4,1)} %get-tuple-element.50) | copy-start | bytes 100
  108.9 3.0 %copy-start.26 = (pred[32]{0:T(512)(128)(4,1)S(1)}, pred[32]{0:T(512)(128)(4,1)}, u32[]{:S(2)}) copy-start(pred[32]{0:T(512)(128)(4,1)} %get-tuple-element.51) | copy-start | bytes 100
  129.8 52.8 %all-to-all-start.3 = ((bf16[32,64,512]{2,1,0:T(8,128)(2,1)}), bf16[32,64,512]{2,1,0:T(8,128)(2,1)}, u32[]{:S(2)}, u32[]{:S(2)}) async-start(bf16[32,64,512]{2,1,0:T(8,128)(2,1)} %add_convert_fusion.1), calls=%async_computation.3 | async-start | bytes 4194304 | tf_op jit(solution)/shard_map/all_to_all | solution.py:178
  167.3 24.1 %copy-start.5 = (bf16[2,64,2,4,640]{4,1,3,2,0:T(8,128)(2,1)S(1)}, bf16[2,64,2,4,640]{4,1,3,2,0:T(8,128)(2,1)}, u32[]{:S(2)}) copy-start(bf16[2,64,2,4,640]{4,1,3,2,0:T(8,128)(2,1)} %copy-done.4) | copy-start | bytes 3932164
  167.3 24.1 %copy-start.18 = (bf16[2,2,128,128]{3,2,0,1:T(8,128)(2,1)S(1)}, bf16[2,2,128,128]{3,2,0,1:T(8,128)(2,1)}, u32[]{:S(2)}) copy-start(bf16[2,2,128,128]{3,2,0,1:T(8,128)(2,1)} %copy-done.17) | copy-start | bytes 393220
  182.7 53.5 %all-to-all-start.4 = ((bf16[32,64,512]{2,1,0:T(8,128)(2,1)}), bf16[32,64,512]{2,1,0:T(8,128)(2,1)S(1)}, u32[]{:S(2)}, u32[]{:S(2)}) async-start(bf16[32,64,512]{2,1,0:T(8,128)(2,1)} %add_convert_fusion), calls=%async_computation.4 | async-start | bytes 4194304 | tf_op jit(solution)/shard_map/all_to_all | solution.py:178
  193.0 8.1 %copy-start.7 = (bf16[2,64,2,4,640]{4,1,3,2,0:T(8,128)(2,1)S(1)}, bf16[2,64,2,4,640]{4,1,3,2,0:T(8,128)(2,1)}, u32[]{:S(2)}) copy-start(bf16[2,64,2,4,640]{4,1,3,2,0:T(8,128)(2,1)} %copy-done.6) | copy-start | bytes 3932164
  202.7 2.9 %copy-start.11 = (bf16[128,1024]{1,0:T(8,128)(2,1)S(1)}, bf16[128,1024]{1,0:T(8,128)(2,1)}, u32[]{:S(2)}) copy-start(bf16[128,1024]{1,0:T(8,128)(2,1)} %reshape.452) | copy-start | bytes 786436
  202.7 17.5 %copy-start.30 = (s32[32]{0:T(128)S(1)}, s32[32]{0:T(128)}, u32[]{:S(2)}) copy-start(s32[32]{0:T(128)} %get-tuple-element.44) | copy-start | bytes 388
  209.5 35.7 %collective-permute-start = (bf16[128,3072]{1,0:T(8,128)(2,1)}, bf16[128,3072]{1,0:T(8,128)(2,1)}, u32[]{:S(2)}, u32[]{:S(2)}) collective-permute-start(bf16[128,3072]{1,0:T(8,128)(2,1)} %constant_dynamic-update-slice_fusion.2), channel_id=1, source_target_pairs={{0,224},{32,0},{64,32},{96,64},{128,96},{160,128},{192,160},{224,1... | collective-permute-start | bytes 2359304 | tf_op jit(solution)/shard_map/ppermute | solution.py:190
  223.0 24.3 %collective-permute-start.1 = (f32[8,64,512]{2,0,1:T(8,128)S(1)}, f32[8,64,512]{2,0,1:T(8,128)}, u32[]{:S(2)}, u32[]{:S(2)}) collective-permute-start(f32[8,64,512]{2,0,1:T(8,128)S(1)} %fusion.8), channel_id=1, source_target_pairs={{0,256},{256,0},{1,257},{257,1},{2,258},{258,2},{3,259},{259,3},{4... | collective-permute-start | bytes 3145736 | tf_op jit(solution)/shard_map/ppermute | solution.py:184
  237.4 11.4 %collective-permute-start.2 = (f32[8,64,512]{2,0,1:T(8,128)S(1)}, f32[8,64,512]{2,0,1:T(8,128)S(1)}, u32[]{:S(2)}, u32[]{:S(2)}) collective-permute-start(f32[8,64,512]{2,0,1:T(8,128)S(1)} %fusion.6), channel_id=1, source_target_pairs={{0,256},{256,0},{1,257},{257,1},{2,258},{258,2},{3,259},{259,3},{4... | collective-permute-start | bytes 3145736 | tf_op jit(solution)/shard_map/ppermute | solution.py:184
  (17 other events, 20.9 us)

commit v6 on v3

--- a/solution.py
+++ b/solution.py
@@ -180,8 +180,10 @@
         owned = jnp.einsum(
             "rj,rtx->jtx", wanted_hot, received, preferred_element_type=jnp.float32
         )
+        if chunk + 1 == chunks:
+            owned = owned.astype(jnp.bfloat16)
         partner = lax.ppermute(owned, "dp", [(0, 1), (1, 0)])
-        owned_parts.append(owned + partner)
+        owned_parts.append(owned.astype(jnp.float32) + partner.astype(jnp.float32))
     section_grads = jnp.concatenate(query_parts + key_parts + value_parts, axis=-1).astype(
         jnp.bfloat16
     )

time: 252 us -> 252 us (level)
  transfers between devices with their start and end apart: 8 -> 8, of which waited for: 5 -> 5; matrix products, arithmetic and copies ran while one was open for 41% -> 40% of each run, Pallas kernels for 0% -> 0%
where the time goes in v6:
time: 252 us; the launch traced here: 250 us
  local copies, waits for them, and re-layouts  72.3 us (29%)
  waiting for transfers between devices  71.1 us (28%)
  starting transfers between devices  63.4 us (25%)
  other arithmetic  26.6 us (11%)
  matrix products  14.5 us (6%)
    all_to_all x2, waiting for transfers between devices, per_device(): lax.all_to_all(payload, 'mem', split_axis=0, concat_axis=0, tiled=True)  42 us
    all_to_all x2, waiting for transfers between devices, per_device(): lax.all_to_all(sent_grads[chunk], 'mem', split_axis=0, concat_axis=0, til...  22.6 us
    all_to_all x2, starting transfers between devices, per_device(): lax.all_to_all(sent_grads[chunk], 'mem', split_axis=0, concat_axis=0, til...  17 us
    ppermute x2, starting transfers between devices, per_device(): partner = lax.ppermute(owned, 'dp', [(0, 1), (1, 0)])  13.6 us
    convert_element_type x2, other arithmetic, per_device(): slot_grads = sum((jnp.where(present[block][:, None, None], by_block[block...  12.1 us
    gather x4, local copies, waits for them, and re-layouts, per_device(): by_block[block].at[key_slot[block]].get(mode='promise_in_bounds')  11.8 us
    all_to_all x2, starting transfers between devices, per_device(): lax.all_to_all(payload, 'mem', split_axis=0, concat_axis=0, tiled=True)  11.7 us
    ppermute x1, starting transfers between devices, per_device(): lax.ppermute(section_grads, 'section', [(i, (i - 1) % sections) for i in...  10.7 us
  transfers between devices with their start and end apart: 8, of which 5 were waited for; matrix products, arithmetic and copies ran while one was open for 40% of the time, Pallas kernels for 0%

profile of v6, /device:TPU:1, one launch (start us, length us, event | category | flops | bytes accessed | tf_op | source)
XLA Modules:
  0.0 250.1 jit_solution(1687156278249814155)
XLA Ops:
  3.3 10.5 %all-to-all-start = ((s32[32,1,2]{2,1,0:T(1,128)}), s32[32,1,2]{2,1,0:T(1,128)S(1)}, u32[]{:S(2)}, u32[]{:S(2)}) async-start(s32[32,1,2]{2,1,0:T(1,128)} %copy.89), calls=%async_computation | async-start | bytes 32768 | tf_op jit(solution)/shard_map/all_to_all | solution.py:100
  15.9 6.5 %all-to-all-done = s32[32,1,2]{2,1,0:T(1,128)S(1)} async-done(((s32[32,1,2]{2,1,0:T(1,128)}), s32[32,1,2]{2,1,0:T(1,128)S(1)}, u32[]{:S(2)}, u32[]{:S(2)}) %all-to-all-start) | async-done | bytes 288 | tf_op jit(solution)/shard_map/all_to_all | solution.py:100
  25.1 4.1 %all-to-all-start.1 = ((bf16[32,64,512]{2,1,0:T(8,128)(2,1)}), bf16[32,64,512]{2,1,0:T(8,128)(2,1)S(1)}, u32[]{:S(2)}, u32[]{:S(2)}) async-start(bf16[32,64,512]{2,1,0:T(8,128)(2,1)} %gather_fusion), calls=%async_computation.1 | async-start | bytes 4194304 | tf_op jit(solution)/shard_map/all_to_all | solution.py:129
  32.6 2.2 reshape_squeeze.3
  46.1 30.2 %all-to-all-done.1 = bf16[32,64,512]{2,1,0:T(8,128)(2,1)S(1)} async-done(((bf16[32,64,512]{2,1,0:T(8,128)(2,1)}), bf16[32,64,512]{2,1,0:T(8,128)(2,1)S(1)}, u32[]{:S(2)}, u32[]{:S(2)}) %all-to-all-start.1) | async-done | bytes 2097184 | tf_op jit(solution)/shard_map/all_to_all | solution.py:129
  76.3 7.6 %all-to-all-start.2 = ((bf16[32,64,512]{2,1,0:T(8,128)(2,1)}), bf16[32,64,512]{2,1,0:T(8,128)(2,1)}, u32[]{:S(2)}, u32[]{:S(2)}) async-start(bf16[32,64,512]{2,1,0:T(8,128)(2,1)} %gather_fusion.3), calls=%async_computation.2 | async-start | bytes 4194304 | tf_op jit(solution)/shard_map/all_to_all | solution.py:129
  95.9 3.0 %reshape.409 = f32[16,64,256]{2,1,0:T(8,128)} reshape(f32[2,512,2,128]{3,2,1,0:T(2,128)} %copy.98) | data formatting | bytes 2097152 | tf_op jit(solution)/shard_map/reshape | solution.py:161
  105.4 3.0 %gather_fusion.4 = f32[32,64,512]{2,1,0:T(8,128)} fusion(f32[8,64,512]{2,1,0:T(8,128)S(1)} %get-tuple-element.20, s32[1024]{0:T(1024)} %get-tuple-element.59), kind=kCustom, calls=%fused_computation.4 | custom fusion | bytes 8388736 | tf_op jit(solution)/shard_map/gather | solution.py:170
  108.4 3.0 %gather_fusion.5 = f32[32,64,512]{2,1,0:T(8,128)} fusion(f32[8,64,512]{2,1,0:T(8,128)S(1)} %get-tuple-element.21, s32[1024]{0:T(1024)} %get-tuple-element.58), kind=kCustom, calls=%fused_computation.5 | custom fusion | bytes 8388736 | tf_op jit(solution)/shard_map/gather | solution.py:170
  111.4 6.1 %add_convert_fusion.1 = bf16[32,64,512]{2,1,0:T(8,128)(2,1)} fusion(f32[32,64,512]{2,1,0:T(8,128)} %gather_fusion.5, f32[32,64,512]{2,1,0:T(8,128)} %gather_fusion.4, pred[32]{0:T(512)(128)(4,1)S(1)} %copy-done.25, pred[32]{0:T(512)(128)(4,1)S(1)} %copy-done.24), kind=kLoop, calls=%fused_computation.10 | loop fusion | flops 4194304 | bytes 10485824 | tf_op jit(solution)/shard_map/convert_element_type | solution.py:174
  117.5 11.8 %all-to-all-done.2 = bf16[32,64,512]{2,1,0:T(8,128)(2,1)} async-done(((bf16[32,64,512]{2,1,0:T(8,128)(2,1)}), bf16[32,64,512]{2,1,0:T(8,128)(2,1)}, u32[]{:S(2)}, u32[]{:S(2)}) %all-to-all-start.2) | async-done | bytes 2097184 | tf_op jit(solution)/shard_map/all_to_all | solution.py:129
  129.3 8.2 %all-to-all-start.3 = ((bf16[32,64,512]{2,1,0:T(8,128)(2,1)}), bf16[32,64,512]{2,1,0:T(8,128)(2,1)}, u32[]{:S(2)}, u32[]{:S(2)}) async-start(bf16[32,64,512]{2,1,0:T(8,128)(2,1)} %add_convert_fusion.1), calls=%async_computation.3 | async-start | bytes 4194304 | tf_op jit(solution)/shard_map/all_to_all | solution.py:177
  137.5 2.2 gather_fusion.6
  147.6 3.1 %reshape.417 = f32[16,64,256]{2,1,0:T(8,128)} reshape(f32[2,512,2,128]{3,2,1,0:T(2,128)} %copy.116) | data formatting | bytes 2097152 | tf_op jit(solution)/shard_map/reshape | solution.py:161
  154.9 2.9 %gather_fusion.7 = f32[32,64,512]{2,1,0:T(8,128)} fusion(f32[8,64,512]{2,1,0:T(8,128)S(1)} %get-tuple-element.18, s32[1024]{0:T(1024)} %get-tuple-element.59), kind=kCustom, calls=%fused_computation.7 | custom fusion | bytes 8388736 | tf_op jit(solution)/shard_map/gather | solution.py:170
  157.8 3.0 %gather_fusion.8 = f32[32,64,512]{2,1,0:T(8,128)} fusion(f32[8,64,512]{2,1,0:T(8,128)S(1)} %get-tuple-element.19, s32[1024]{0:T(1024)} %get-tuple-element.58), kind=kCustom, calls=%fused_computation.8 | custom fusion | bytes 8388736 | tf_op jit(solution)/shard_map/gather | solution.py:170
  160.8 6.0 %add_convert_fusion = bf16[32,64,512]{2,1,0:T(8,128)(2,1)} fusion(f32[32,64,512]{2,1,0:T(8,128)} %gather_fusion.8, f32[32,64,512]{2,1,0:T(8,128)} %gather_fusion.7, pred[32]{0:T(512)(128)(4,1)S(1)} %copy-done.25, pred[32]{0:T(512)(128)(4,1)S(1)} %copy-done.24), kind=kLoop, calls=%fused_computation.9 | loop fusion | flops 4194304 | bytes 10485824 | tf_op jit(solution)/shard_map/convert_element_type | solution.py:174
  166.8 15.3 %all-to-all-done.3 = bf16[32,64,512]{2,1,0:T(8,128)(2,1)} async-done(((bf16[32,64,512]{2,1,0:T(8,128)(2,1)}), bf16[32,64,512]{2,1,0:T(8,128)(2,1)}, u32[]{:S(2)}, u32[]{:S(2)}) %all-to-all-start.3) | async-done | bytes 2097184 | tf_op jit(solution)/shard_map/all_to_all | solution.py:177
  182.2 8.8 %all-to-all-start.4 = ((bf16[32,64,512]{2,1,0:T(8,128)(2,1)}), bf16[32,64,512]{2,1,0:T(8,128)(2,1)S(1)}, u32[]{:S(2)}, u32[]{:S(2)}) async-start(bf16[32,64,512]{2,1,0:T(8,128)(2,1)} %add_convert_fusion), calls=%async_computation.4 | async-start | bytes 4194304 | tf_op jit(solution)/shard_map/all_to_all | solution.py:177
  209.0 10.7 %collective-permute-start = (bf16[128,3072]{1,0:T(8,128)(2,1)}, bf16[128,3072]{1,0:T(8,128)(2,1)}, u32[]{:S(2)}, u32[]{:S(2)}) collective-permute-start(bf16[128,3072]{1,0:T(8,128)(2,1)} %constant_dynamic-update-slice_fusion.2), channel_id=1, source_target_pairs={{0,224},{32,0},{64,32},{96,64},{128,96},{160,128},{192,160},{224,1... | collective-permute-start | bytes 2359304 | tf_op jit(solution)/shard_map/ppermute | solution.py:191
  219.7 2.8 %fusion.8 = f32[8,64,512]{2,0,1:T(8,128)S(1)} fusion(bf16[32,64,512]{2,1,0:T(8,128)(2,1)} %all-to-all-done.3, s32[32]{0:T(128)S(1)} %copy-done.29), kind=kOutput, calls=%fused_computation.27 | convolution fusion | flops 16777472 | bytes 3145856 | tf_op jit(solution)/shard_map/rj,rtx->jtx/dot_general | solution.py:180
  222.5 5.8 %collective-permute-start.1 = (f32[8,64,512]{2,0,1:T(8,128)S(1)}, f32[8,64,512]{2,0,1:T(8,128)}, u32[]{:S(2)}, u32[]{:S(2)}) collective-permute-start(f32[8,64,512]{2,0,1:T(8,128)S(1)} %fusion.8), channel_id=1, source_target_pairs={{0,256},{256,0},{1,257},{257,1},{2,258},{258,2},{3,259},{259,3},{4... | collective-permute-start | bytes 3145736 | tf_op jit(solution)/shard_map/ppermute | solution.py:185
  228.4 7.3 %all-to-all-done.4 = bf16[32,64,512]{2,1,0:T(8,128)(2,1)S(1)} async-done(((bf16[32,64,512]{2,1,0:T(8,128)(2,1)}), bf16[32,64,512]{2,1,0:T(8,128)(2,1)S(1)}, u32[]{:S(2)}, u32[]{:S(2)}) %all-to-all-start.4) | async-done | bytes 2097184 | tf_op jit(solution)/shard_map/all_to_all | solution.py:177
  236.9 7.8 %collective-permute-start.2 = (bf16[8,64,512]{2,0,1:T(8,128)(2,1)S(1)}, bf16[8,64,512]{2,0,1:T(8,128)(2,1)S(1)}, u32[]{:S(2)}, u32[]{:S(2)}) collective-permute-start(bf16[8,64,512]{2,0,1:T(8,128)(2,1)S(1)} %fusion.14), channel_id=1, source_target_pairs={{0,256},{256,0},{1,257},{257,1},{2,258},{258,2},{3,259},{259,3},{4... | collective-permute-start | bytes 1572872 | tf_op jit(solution)/shard_map/ppermute | solution.py:185
  (189 shorter events, 76.1 us)
Async XLA Ops:
  2.6 13.2 %copy-start.27 = (s32[32]{0:T(128)}, s32[32]{0:T(128)S(1)}, u32[]{:S(2)}) copy-start(s32[32]{0:T(128)S(1)} %get-tuple-element.17) | copy-start | bytes 388
  3.3 19.0 %all-to-all-start = ((s32[32,1,2]{2,1,0:T(1,128)}), s32[32,1,2]{2,1,0:T(1,128)S(1)}, u32[]{:S(2)}, u32[]{:S(2)}) async-start(s32[32,1,2]{2,1,0:T(1,128)} %copy.89), calls=%async_computation | async-start | bytes 32768 | tf_op jit(solution)/shard_map/all_to_all | solution.py:100
  25.1 4.2 %copy-start.30 = (s32[1,1,2,8]{3,2,1,0:T(2,128)S(1)}, s32[1,1,2,8]{3,2,1,0:T(2,128)}, u32[]{:S(2)}) copy-start(s32[1,1,2,8]{3,2,1,0:T(2,128)} %param.9) | copy-start | bytes 196
  25.1 51.2 %all-to-all-start.1 = ((bf16[32,64,512]{2,1,0:T(8,128)(2,1)}), bf16[32,64,512]{2,1,0:T(8,128)(2,1)S(1)}, u32[]{:S(2)}, u32[]{:S(2)}) async-start(bf16[32,64,512]{2,1,0:T(8,128)(2,1)} %gather_fusion), calls=%async_computation.1 | async-start | bytes 4194304 | tf_op jit(solution)/shard_map/all_to_all | solution.py:129
  29.4 5.4 %copy-start.26 = (s32[2,32]{1,0:T(2,128)S(1)}, s32[2,32]{1,0:T(2,128)}, u32[]{:S(2)}) copy-start(s32[2,32]{1,0:T(2,128)} %get-tuple-element.16) | copy-start | bytes 772
  34.8 6.4 %copy-start.10 = (bf16[2,64,4,4,128]{4,3,2,1,0:T(4,128)(2,1)S(1)}, bf16[2,64,4,4,128]{4,3,2,1,0:T(4,128)(2,1)}, u32[]{:S(2)}) copy-start(bf16[2,64,4,4,128]{4,3,2,1,0:T(4,128)(2,1)} %reshape_squeeze.3) | copy-start | bytes 1572868
  35.5 5.9 %copy-start.28 = (s32[32]{0:T(128)S(1)}, s32[32]{0:T(128)}, u32[]{:S(2)}) copy-start(s32[32]{0:T(128)} %copy-done.27) | copy-start | bytes 388
  35.5 5.9 %copy-start.32 = (s32[32,1,2]{0,2,1:T(2,128)S(1)}, s32[32,1,2]{0,2,1:T(2,128)}, u32[]{:S(2)}) copy-start(s32[32,1,2]{0,2,1:T(2,128)} %copy-done.31) | copy-start | bytes 772
  46.1 37.7 %copy-start.33 = (s32[2,8]{1,0:T(2,128)S(1)}, s32[2,8]{1,0:T(2,128)}, u32[]{:S(2)}) copy-start(s32[2,8]{1,0:T(2,128)} %gather.33) | copy-start | bytes 196
  46.1 37.9 %copy-start.22 = (pred[2,64,128]{2,1,0:T(8,128)(4,1)S(1)}, pred[2,64,128]{2,1,0:T(8,128)(4,1)}, u32[]{:S(2)}) copy-start(pred[2,64,128]{2,1,0:T(8,128)(4,1)} %iota_compare_fusion) | copy-start | bytes 49156
  76.3 53.0 %all-to-all-start.2 = ((bf16[32,64,512]{2,1,0:T(8,128)(2,1)}), bf16[32,64,512]{2,1,0:T(8,128)(2,1)}, u32[]{:S(2)}, u32[]{:S(2)}) async-start(bf16[32,64,512]{2,1,0:T(8,128)(2,1)} %gather_fusion.3), calls=%async_computation.2 | async-start | bytes 4194304 | tf_op jit(solution)/shard_map/all_to_all | solution.py:129
  101.1 3.9 %copy-start.8 = (f32[16,64,256]{2,1,0:T(8,128)S(1)}, f32[16,64,256]{2,1,0:T(8,128)}, u32[]{:S(2)}) copy-start(f32[16,64,256]{2,1,0:T(8,128)} %reshape.409) | copy-start | bytes 3145732
  108.4 3.0 %copy-start.24 = (pred[32]{0:T(512)(128)(4,1)S(1)}, pred[32]{0:T(512)(128)(4,1)}, u32[]{:S(2)}) copy-start(pred[32]{0:T(512)(128)(4,1)} %get-tuple-element.50) | copy-start | bytes 100
  108.4 3.0 %copy-start.25 = (pred[32]{0:T(512)(128)(4,1)S(1)}, pred[32]{0:T(512)(128)(4,1)}, u32[]{:S(2)}) copy-start(pred[32]{0:T(512)(128)(4,1)} %get-tuple-element.51) | copy-start | bytes 100
  129.3 52.8 %all-to-all-start.3 = ((bf16[32,64,512]{2,1,0:T(8,128)(2,1)}), bf16[32,64,512]{2,1,0:T(8,128)(2,1)}, u32[]{:S(2)}, u32[]{:S(2)}) async-start(bf16[32,64,512]{2,1,0:T(8,128)(2,1)} %add_convert_fusion.1), calls=%async_computation.3 | async-start | bytes 4194304 | tf_op jit(solution)/shard_map/all_to_all | solution.py:177
  166.8 24.1 %copy-start.5 = (bf16[2,64,2,4,640]{4,1,3,2,0:T(8,128)(2,1)S(1)}, bf16[2,64,2,4,640]{4,1,3,2,0:T(8,128)(2,1)}, u32[]{:S(2)}) copy-start(bf16[2,64,2,4,640]{4,1,3,2,0:T(8,128)(2,1)} %copy-done.4) | copy-start | bytes 3932164
  166.8 24.1 %copy-start.18 = (bf16[2,2,128,128]{3,2,0,1:T(8,128)(2,1)S(1)}, bf16[2,2,128,128]{3,2,0,1:T(8,128)(2,1)}, u32[]{:S(2)}) copy-start(bf16[2,2,128,128]{3,2,0,1:T(8,128)(2,1)} %copy-done.17) | copy-start | bytes 393220
  182.2 53.5 %all-to-all-start.4 = ((bf16[32,64,512]{2,1,0:T(8,128)(2,1)}), bf16[32,64,512]{2,1,0:T(8,128)(2,1)S(1)}, u32[]{:S(2)}, u32[]{:S(2)}) async-start(bf16[32,64,512]{2,1,0:T(8,128)(2,1)} %add_convert_fusion), calls=%async_computation.4 | async-start | bytes 4194304 | tf_op jit(solution)/shard_map/all_to_all | solution.py:177
  192.5 8.1 %copy-start.7 = (bf16[2,64,2,4,640]{4,1,3,2,0:T(8,128)(2,1)S(1)}, bf16[2,64,2,4,640]{4,1,3,2,0:T(8,128)(2,1)}, u32[]{:S(2)}) copy-start(bf16[2,64,2,4,640]{4,1,3,2,0:T(8,128)(2,1)} %copy-done.6) | copy-start | bytes 3932164
  202.2 2.9 %copy-start.11 = (bf16[128,1024]{1,0:T(8,128)(2,1)S(1)}, bf16[128,1024]{1,0:T(8,128)(2,1)}, u32[]{:S(2)}) copy-start(bf16[128,1024]{1,0:T(8,128)(2,1)} %reshape.408) | copy-start | bytes 786436
  202.2 17.5 %copy-start.29 = (s32[32]{0:T(128)S(1)}, s32[32]{0:T(128)}, u32[]{:S(2)}) copy-start(s32[32]{0:T(128)} %get-tuple-element.44) | copy-start | bytes 388
  209.0 35.7 %collective-permute-start = (bf16[128,3072]{1,0:T(8,128)(2,1)}, bf16[128,3072]{1,0:T(8,128)(2,1)}, u32[]{:S(2)}, u32[]{:S(2)}) collective-permute-start(bf16[128,3072]{1,0:T(8,128)(2,1)} %constant_dynamic-update-slice_fusion.2), channel_id=1, source_target_pairs={{0,224},{32,0},{64,32},{96,64},{128,96},{160,128},{192,160},{224,1... | collective-permute-start | bytes 2359304 | tf_op jit(solution)/shard_map/ppermute | solution.py:191
  222.5 24.5 %collective-permute-start.1 = (f32[8,64,512]{2,0,1:T(8,128)S(1)}, f32[8,64,512]{2,0,1:T(8,128)}, u32[]{:S(2)}, u32[]{:S(2)}) collective-permute-start(f32[8,64,512]{2,0,1:T(8,128)S(1)} %fusion.8), channel_id=1, source_target_pairs={{0,256},{256,0},{1,257},{257,1},{2,258},{258,2},{3,259},{259,3},{4... | collective-permute-start | bytes 3145736 | tf_op jit(solution)/shard_map/ppermute | solution.py:185
  236.9 9.9 %collective-permute-start.2 = (bf16[8,64,512]{2,0,1:T(8,128)(2,1)S(1)}, bf16[8,64,512]{2,0,1:T(8,128)(2,1)S(1)}, u32[]{:S(2)}, u32[]{:S(2)}) collective-permute-start(bf16[8,64,512]{2,0,1:T(8,128)(2,1)S(1)} %fusion.14), channel_id=1, source_target_pairs={{0,256},{256,0},{1,257},{257,1},{2,258},{258,2},{3,259},{259,3},{4... | collective-permute-start | bytes 1572872 | tf_op jit(solution)/shard_map/ppermute | solution.py:185
  (18 other events, 23.0 us)
